TPU v7x, 256 devices: a whole 4x4x8 slice. The times are simulated.
256 devices in a mesh: dp: 16 (over y_hi, z), seq: 16 (over x, y_lo, core).
Axes of the slice: x: 4, y: 4 (y_hi: 2, y_lo: 2; y = y_hi * 2 + y_lo), z: 8, core: 2. Of those that a mesh axis runs over, the one named last changes fastest.
Arguments:
- queries: bfloat16 [16, 2048, 2048], P('dp', 'seq'), may hold values from -6 to 6
- key_states: bfloat16 [16, 2048, 2048], P('dp', 'seq'), may hold values from -6 to 6
- value_states: bfloat16 [16, 2048, 2048], P('dp', 'seq'), may hold values from -6 to 6
- cotangent: bfloat16 [16, 2048, 2048], P('dp', 'seq'), may hold values from -6 to 6
- filter_taps: float32 [7, 2048], replicated, may hold values from -3 to 3
Outputs:
- conv_output: bfloat16 [16, 2048, 2048], P('dp', 'seq')
- grad_queries: bfloat16 [16, 2048, 2048], P('dp', 'seq')
- grad_keys: bfloat16 [16, 2048, 2048], P('dp', 'seq')
- grad_values: bfloat16 [16, 2048, 2048], P('dp', 'seq')
- filter_gradient: float32 [7, 2048], replicated
All inputs are finite; a program needn't handle non-finite values.
Results may differ from a plain program's by a relative error of at most 0.015.
Values may be sent and summed in bfloat16 or wider, within the bound.
No kernel may reach another device: no remote copies, remote signals or barrier semaphores. Data moves between devices by JAX's collectives and lax.ppermute only.
A program may use at most 128 MiB of HBM per device.

v0:
```python
import math

import jax
import jax.numpy as jnp
from jax import lax
from jax.sharding import PartitionSpec as P

HD = 128
TAPS = 7


def padded(value, sides, width):
    for axis, dim in sides:
        peers, length = (lax.axis_size(axis), value.shape[dim])
        up = [(i, (i + 1) % peers) for i in range(peers)]
        down = [(j, i) for i, j in up]
        last = lax.slice_in_dim(value, length - width, length, axis=dim)
        leading = lax.slice_in_dim(value, 0, width, axis=dim)
        before = lax.ppermute(last, axis, up)
        after = lax.ppermute(leading, axis, down)
        value = jnp.concatenate([before, value, after], axis=dim)
    return value


def on_device(queries, key_states, value_states, cotangent, filter_taps):
    tok_rows = queries.shape[1]
    channels = queries.shape[2]
    sequence_shards = lax.axis_size("seq")
    seq_total = tok_rows * sequence_shards
    head_count = channels // HD
    group_heads = math.gcd(head_count, 4)
    group_width = group_heads * HD
    group_count = head_count // group_heads
    score_scale = HD ** (-0.5)
    half_width = (TAPS - 1) // 2
    local_q = queries[0]
    local_k = key_states[0]
    local_v = value_states[0]
    local_g = cotangent[0]
    grad_pad = padded(local_g, (("seq", 0),), half_width)
    grad_sum = jnp.zeros((tok_rows, channels), jnp.float32)
    for tap_index in range(TAPS):
        start_row = 2 * half_width - tap_index
        grad_sum = grad_sum + filter_taps[tap_index] * grad_pad[
            start_row : start_row + tok_rows
        ].astype(jnp.float32)
    grad_attn = grad_sum.astype(jnp.bfloat16)
    key_all, value_all = (
        lax.all_gather(local_k, "seq", axis=0, tiled=True),
        lax.all_gather(local_v, "seq", axis=0, tiled=True),
    )
    device_index = lax.axis_index("seq")
    query_pos = device_index * tok_rows + jnp.arange(tok_rows, dtype=jnp.int32)
    key_pos = jnp.arange(seq_total, dtype=jnp.int32)
    visible = query_pos[:, None] >= key_pos[None, :]

    def columns(matrix, group_index, count):
        picked = lax.dynamic_slice_in_dim(matrix, group_index * group_width, group_width, 1)
        return picked.reshape(count, group_heads, HD)

    def forward_group(group_index):
        q_part = columns(local_q, group_index, tok_rows)
        k_part = columns(key_all, group_index, seq_total)
        v_part = columns(value_all, group_index, seq_total)
        delta_portion = columns(grad_attn, group_index, tok_rows)
        scores = (
            jnp.einsum("thd,uhd->htu", q_part, k_part, preferred_element_type=jnp.float32)
            * score_scale
        )
        row_top = jnp.max(jnp.where(visible, scores, -jnp.inf), -1, keepdims=True)
        raw = jnp.where(visible, jnp.exp(scores - row_top), 0.0)
        row_total = jnp.sum(raw, -1, keepdims=True)
        probs = raw / row_total
        probs_low = probs.astype(jnp.bfloat16)
        attended = jnp.einsum("htu,uhd->thd", probs_low, v_part, preferred_element_type=jnp.float32)
        attended = attended.astype(jnp.bfloat16).reshape(tok_rows, group_width)
        dprob = jnp.einsum(
            "thd,uhd->htu", delta_portion, v_part, preferred_element_type=jnp.float32
        )
        row_delta = jnp.sum(probs * dprob, -1, keepdims=True)
        dscore = (probs * (dprob - row_delta) * score_scale).astype(jnp.bfloat16)
        grad_q = jnp.einsum("htu,uhd->thd", dscore, k_part, preferred_element_type=jnp.float32)
        grad_q = grad_q.astype(jnp.bfloat16).reshape(tok_rows, group_width)
        key_term = jnp.einsum("htu,thd->uhd", dscore, q_part, preferred_element_type=jnp.float32)
        value_term = jnp.einsum(
            "htu,thd->uhd", probs_low, delta_portion, preferred_element_type=jnp.float32
        )
        return (
            attended,
            grad_q,
            key_term.reshape(seq_total, group_width),
            value_term.reshape(seq_total, group_width),
        )

    group_ids = jnp.arange(group_count, dtype=jnp.int32)
    attended, grad_q, key_term, value_term = lax.map(forward_group, group_ids)
    key_share, value_share = (
        lax.psum_scatter(
            key_term.astype(jnp.bfloat16), "seq", scatter_dimension=1, tiled=True
        ).astype(jnp.float32),
        lax.psum_scatter(
            value_term.astype(jnp.bfloat16), "seq", scatter_dimension=1, tiled=True
        ).astype(jnp.float32),
    )
    grad_keys = key_share.transpose(1, 0, 2).reshape(tok_rows, channels).astype(jnp.bfloat16)
    grad_values = value_share.transpose(1, 0, 2).reshape(tok_rows, channels).astype(jnp.bfloat16)
    attn_out = attended.transpose(1, 0, 2).reshape(tok_rows, channels)
    grad_queries = grad_q.transpose(1, 0, 2).reshape(tok_rows, channels)
    out_pad = padded(attn_out, (("seq", 0),), half_width)
    conv_sum = jnp.zeros((tok_rows, channels), jnp.float32)
    filter_rows = []
    local_gf = local_g.astype(jnp.float32)
    for tap_index in range(TAPS):
        moved = out_pad[tap_index : tap_index + tok_rows].astype(jnp.float32)
        conv_sum = conv_sum + filter_taps[tap_index] * moved
        filter_rows.append(jnp.sum(moved * local_gf, 0))
    filter_gradient = lax.psum(jnp.stack(filter_rows, 0), ("dp", "seq"))
    conv_output = conv_sum.astype(jnp.bfloat16)
    return (
        conv_output[None],
        grad_queries[None],
        grad_keys[None],
        grad_values[None],
        filter_gradient,
    )


def solution(mesh):
    in_specs = (
        P("dp", "seq", None),
        P("dp", "seq", None),
        P("dp", "seq", None),
        P("dp", "seq", None),
        P(),
    )
    out_specs = (
        P("dp", "seq", None),
        P("dp", "seq", None),
        P("dp", "seq", None),
        P("dp", "seq", None),
        P(),
    )
    return jax.shard_map(
        on_device, mesh=mesh, in_specs=in_specs, out_specs=out_specs, check_vma=False
    )
```

profile of v0, /device:TPU:1, one launch (start us, length us, event | category | flops | bytes accessed | tf_op | source)
XLA Modules:
  0.0 557.8 jit_solution(18201332075401801703)
XLA Ops:
  7.2 2.1 copy.41
  9.4 2.0 copy.43
  12.3 2.8 collective-permute-start.1
  17.1 2.0 copy.42
  19.1 1.7 fusion.47
  20.9 57.9 %all-gather.5.cloned.1.call-done = bf16[1,2048,2048]{1,2,0:T(8,128)(2,1)} async-done(((bf16[1,128,2048]{1,2,0:T(8,128)(2,1)}), bf16[1,2048,2048]{1,2,0:T(8,128)(2,1)}) %all-gather.5.cloned.1.call-update) | async-done | bytes 8388624 | tf_op jit(solution)/shard_map/all_gather | solution.py:50
  78.7 65.4 %all-gather.7.cloned.1.call-done = bf16[1,2048,2048]{1,2,0:T(8,128)(2,1)} async-done(((bf16[1,128,2048]{1,2,0:T(8,128)(2,1)}), bf16[1,2048,2048]{1,2,0:T(8,128)(2,1)}) %all-gather.7.cloned.1.call-update) | async-done | bytes 8388624 | tf_op jit(solution)/shard_map/all_gather | solution.py:49
  144.2 177.4 %while.17 = (s32[]{:T(128)}, bf16[4,128,512]{1,2,0:T(8,128)(2,1)S(1)}, bf16[4,128,512]{1,2,0:T(8,128)(2,1)}, bf16[4,2048,512]{1,2,0:T(8,128)(2,1)}, bf16[4,2048,...) while((s32[]{:T(128)}, ...), condition=%wide.region_4.5_spmd.clone, body=%wide.region_0.4_spmd.clone.sunk | while | flops 1904614400 | bytes 82324224 | solution.py:96
  145.5 3.2 constant_dynamic-slice_fusion.8
  149.7 1.7 constant_dynamic-slice_fusion.10
  151.5 2.8 fusion.110
  155.4 6.5 %fusion.111 = (f32[4,128]{1,0:T(4,128)S(1)}, f32[4,128,2048]{2,1,0:T(8,128)}) fusion(pred[128,2048]{1,0:T(8,128)(4,1)S(1)} %iota_compare_fusion.2, bf16[128,4,128]{0,2,1:T(8,128)(2,1)S(1)} %bitcast.143, bf16[2048,4,128]{0,2,1:T(8,128)(2,1)} %bitcast.125), kind=kOutput, calls=%fused_computation.95.clone.1 | convolution fusion | flops 543164416 | bytes 6686720 | tf_op jit(solution)/shard_map/while/body/eval_jaxpr/sub | solution.py:71
  161.9 8.5 %fusion.112 = bf16[4,128,128]{2,1,0:T(8,128)(2,1)S(1)} fusion(bf16[2048,4,128]{0,2,1:T(8,128)(2,1)} %bitcast.126, f32[4,128,2048]{2,1,0:T(8,128)} %fusion.110, f32[4,128,2048]{2,1,0:T(8,128)} %get-tuple-element.242, f32[4,128]{1,0:T(4,128)S(1)} %get-tuple-element.243), kind=kOutput, calls=%fused_computation.18.clone.1 | convolution fusion | flops 275843584 | bytes 10618880 | tf_op jit(solution)/shard_map/while/body/eval_jaxpr/htu,uhd->thd/dot_general | solution.py:82
  170.5 3.1 convolution_convert_fusion.2
  175.1 9.5 %fusion.114 = bf16[4,128,2048]{2,1,0:T(8,128)(2,1)} fusion(bf16[128,4,128]{0,2,1:T(8,128)(2,1)S(1)} %bitcast.144, f32[4,128,2048]{2,1,0:T(8,128)} %fusion.110, f32[4,128,2048]{2,1,0:T(8,128)} %get-tuple-element.242, f32[4,128]{1,0:T(4,128)S(1)} %get-tuple-element.243), kind=kOutput, calls=%fused_computation.10.clone.1 | convolution fusion | flops 275778048 | bytes 10618880 | tf_op jit(solution)/shard_map/while/body/eval_jaxpr/htu,thd->uhd/dot_general | solution.py:84
  184.6 4.0 constant_dynamic-update-slice_fusion.7
  189.8 3.2 constant_dynamic-slice_fusion.8
  194.1 1.7 constant_dynamic-slice_fusion.10
  195.8 2.8 fusion.110
  199.7 6.5 %fusion.111 = (f32[4,128]{1,0:T(4,128)S(1)}, f32[4,128,2048]{2,1,0:T(8,128)}) fusion(pred[128,2048]{1,0:T(8,128)(4,1)S(1)} %iota_compare_fusion.2, bf16[128,4,128]{0,2,1:T(8,128)(2,1)S(1)} %bitcast.143, bf16[2048,4,128]{0,2,1:T(8,128)(2,1)} %bitcast.125), kind=kOutput, calls=%fused_computation.95.clone.1 | convolution fusion | flops 543164416 | bytes 6686720 | tf_op jit(solution)/shard_map/while/body/eval_jaxpr/sub | solution.py:71
  206.3 8.5 %fusion.112 = bf16[4,128,128]{2,1,0:T(8,128)(2,1)S(1)} fusion(bf16[2048,4,128]{0,2,1:T(8,128)(2,1)} %bitcast.126, f32[4,128,2048]{2,1,0:T(8,128)} %fusion.110, f32[4,128,2048]{2,1,0:T(8,128)} %get-tuple-element.242, f32[4,128]{1,0:T(4,128)S(1)} %get-tuple-element.243), kind=kOutput, calls=%fused_computation.18.clone.1 | convolution fusion | flops 275843584 | bytes 10618880 | tf_op jit(solution)/shard_map/while/body/eval_jaxpr/htu,uhd->thd/dot_general | solution.py:82
  214.8 3.1 convolution_convert_fusion.2
  219.4 9.5 %fusion.114 = bf16[4,128,2048]{2,1,0:T(8,128)(2,1)} fusion(bf16[128,4,128]{0,2,1:T(8,128)(2,1)S(1)} %bitcast.144, f32[4,128,2048]{2,1,0:T(8,128)} %fusion.110, f32[4,128,2048]{2,1,0:T(8,128)} %get-tuple-element.242, f32[4,128]{1,0:T(4,128)S(1)} %get-tuple-element.243), kind=kOutput, calls=%fused_computation.10.clone.1 | convolution fusion | flops 275778048 | bytes 10618880 | tf_op jit(solution)/shard_map/while/body/eval_jaxpr/htu,thd->uhd/dot_general | solution.py:84
  228.9 4.0 constant_dynamic-update-slice_fusion.7
  234.2 3.2 constant_dynamic-slice_fusion.8
  238.4 1.7 constant_dynamic-slice_fusion.10
  240.1 2.8 fusion.110
  244.1 6.5 %fusion.111 = (f32[4,128]{1,0:T(4,128)S(1)}, f32[4,128,2048]{2,1,0:T(8,128)}) fusion(pred[128,2048]{1,0:T(8,128)(4,1)S(1)} %iota_compare_fusion.2, bf16[128,4,128]{0,2,1:T(8,128)(2,1)S(1)} %bitcast.143, bf16[2048,4,128]{0,2,1:T(8,128)(2,1)} %bitcast.125), kind=kOutput, calls=%fused_computation.95.clone.1 | convolution fusion | flops 543164416 | bytes 6686720 | tf_op jit(solution)/shard_map/while/body/eval_jaxpr/sub | solution.py:71
  250.6 8.5 %fusion.112 = bf16[4,128,128]{2,1,0:T(8,128)(2,1)S(1)} fusion(bf16[2048,4,128]{0,2,1:T(8,128)(2,1)} %bitcast.126, f32[4,128,2048]{2,1,0:T(8,128)} %fusion.110, f32[4,128,2048]{2,1,0:T(8,128)} %get-tuple-element.242, f32[4,128]{1,0:T(4,128)S(1)} %get-tuple-element.243), kind=kOutput, calls=%fused_computation.18.clone.1 | convolution fusion | flops 275843584 | bytes 10618880 | tf_op jit(solution)/shard_map/while/body/eval_jaxpr/htu,uhd->thd/dot_general | solution.py:82
  259.2 3.1 convolution_convert_fusion.2
  263.8 9.5 %fusion.114 = bf16[4,128,2048]{2,1,0:T(8,128)(2,1)} fusion(bf16[128,4,128]{0,2,1:T(8,128)(2,1)S(1)} %bitcast.144, f32[4,128,2048]{2,1,0:T(8,128)} %fusion.110, f32[4,128,2048]{2,1,0:T(8,128)} %get-tuple-element.242, f32[4,128]{1,0:T(4,128)S(1)} %get-tuple-element.243), kind=kOutput, calls=%fused_computation.10.clone.1 | convolution fusion | flops 275778048 | bytes 10618880 | tf_op jit(solution)/shard_map/while/body/eval_jaxpr/htu,thd->uhd/dot_general | solution.py:84
  273.3 4.0 constant_dynamic-update-slice_fusion.7
  278.5 3.2 constant_dynamic-slice_fusion.8
  282.7 1.7 constant_dynamic-slice_fusion.10
  284.5 2.8 fusion.110
  288.4 6.5 %fusion.111 = (f32[4,128]{1,0:T(4,128)S(1)}, f32[4,128,2048]{2,1,0:T(8,128)}) fusion(pred[128,2048]{1,0:T(8,128)(4,1)S(1)} %iota_compare_fusion.2, bf16[128,4,128]{0,2,1:T(8,128)(2,1)S(1)} %bitcast.143, bf16[2048,4,128]{0,2,1:T(8,128)(2,1)} %bitcast.125), kind=kOutput, calls=%fused_computation.95.clone.1 | convolution fusion | flops 543164416 | bytes 6686720 | tf_op jit(solution)/shard_map/while/body/eval_jaxpr/sub | solution.py:71
  294.9 8.5 %fusion.112 = bf16[4,128,128]{2,1,0:T(8,128)(2,1)S(1)} fusion(bf16[2048,4,128]{0,2,1:T(8,128)(2,1)} %bitcast.126, f32[4,128,2048]{2,1,0:T(8,128)} %fusion.110, f32[4,128,2048]{2,1,0:T(8,128)} %get-tuple-element.242, f32[4,128]{1,0:T(4,128)S(1)} %get-tuple-element.243), kind=kOutput, calls=%fused_computation.18.clone.1 | convolution fusion | flops 275843584 | bytes 10618880 | tf_op jit(solution)/shard_map/while/body/eval_jaxpr/htu,uhd->thd/dot_general | solution.py:82
  303.5 3.1 convolution_convert_fusion.2
  308.1 9.5 %fusion.114 = bf16[4,128,2048]{2,1,0:T(8,128)(2,1)} fusion(bf16[128,4,128]{0,2,1:T(8,128)(2,1)S(1)} %bitcast.144, f32[4,128,2048]{2,1,0:T(8,128)} %fusion.110, f32[4,128,2048]{2,1,0:T(8,128)} %get-tuple-element.242, f32[4,128]{1,0:T(4,128)S(1)} %get-tuple-element.243), kind=kOutput, calls=%fused_computation.10.clone.1 | convolution fusion | flops 275778048 | bytes 10618880 | tf_op jit(solution)/shard_map/while/body/eval_jaxpr/htu,thd->uhd/dot_general | solution.py:84
  317.6 4.0 constant_dynamic-update-slice_fusion.7
  321.6 14.6 %copy.60 = bf16[4,2048,512]{2,0,1:T(4,128)(2,1)} copy(bf16[4,2048,512]{1,2,0:T(8,128)(2,1)} %get-tuple-element.67) | data formatting | bytes 16777216
  336.2 10.2 %copy.65 = bf16[256,8,4,512]{3,1,2,0:T(8,128)(2,1)} copy(bf16[256,8,4,512]{3,2,1,0:T(4,128)(2,1)} %bitcast.131) | data formatting | bytes 16777216
  346.5 14.6 %copy.62 = bf16[4,2048,512]{2,0,1:T(4,128)(2,1)} copy(bf16[4,2048,512]{1,2,0:T(8,128)(2,1)} %get-tuple-element.68) | data formatting | bytes 16777216
  361.0 10.2 %copy.66 = bf16[256,8,4,512]{3,1,2,0:T(8,128)(2,1)} copy(bf16[256,8,4,512]{3,2,1,0:T(4,128)(2,1)} %bitcast.132) | data formatting | bytes 16777216
  375.9 2.0 copy.59
  379.1 78.2 %psum.7 = f32[7,2048]{1,0:T(8,128)} all-reduce(f32[7,2048]{1,0:T(8,128)S(1)} %stack.31), channel_id=1, replica_groups=mesh['dp'=16,'seq'=16] {'dp','seq'}, use_global_device_ids=true, to_apply=%region_14.15 | all-reduce | flops 14336 | bytes 114688 | tf_op jit(solution)/shard_map/psum | solution.py:117
  457.4 1.7 fusion.62
  462.0 86.5 %reduce-scatter.9.cloned.1.call-done = bf16[128,2048]{1,0:T(8,128)(2,1)} async-done(((bf16[2048,2048]{1,0:T(8,128)(2,1)}), bf16[128,2048]{1,0:T(8,128)(2,1)}) %reduce-scatter.9.cloned.1.call-update) | async-done | bytes 524304
  (107 shorter events, 31.1 us)
Async XLA Ops:
  7.2 11.9 %copy-start = (bf16[1,128,2048]{2,1,0:T(8,128)(2,1)S(1)}, bf16[1,128,2048]{2,1,0:T(8,128)(2,1)}, u32[]{:S(2)}) copy-start(bf16[1,128,2048]{2,1,0:T(8,128)(2,1)} %param.10) | copy-start | bytes 1572868
  7.2 71.6 %all-gather.5.cloned.1.call-start = ((), (), s32[]{:S(2)}) async-start(), calls=%async_computation.2 | async-start | bytes 8912896 | tf_op jit(solution)/shard_map/all_gather | solution.py:50
  9.3 134.8 %all-gather.7.cloned.1.call-start = ((), (), s32[]{:S(2)}) async-start(), calls=%async_computation.3 | async-start | bytes 8912896 | tf_op jit(solution)/shard_map/all_gather | solution.py:49
  11.5 447.6 %reduce-scatter.7.cloned.1.call-start = ((), (), s32[]{:S(2)}) async-start(), calls=%async_computation.4 | async-start | bytes 8912896
  12.3 6.8 %collective-permute-start.1 = (bf16[3,2048]{1,0:T(4,128)(2,1)S(1)}, bf16[3,2048]{1,0:T(4,128)(2,1)S(1)}, u32[]{:S(2)}, u32[]{:S(2)}) collective-permute-start(bf16[3,2048]{1,0:T(4,128)(2,1)S(1)} %get-tuple-element.161), channel_id=1, source_target_pairs={{0,1},{1,2},{2,3},{3,4},{4,5},{5,6},{6,7},{7,8},{8,9},{9,10},{10,1... | collective-permute-start | bytes 36872 | tf_op jit(solution)/shard_map/ppermute | solution.py:19
  15.1 4.0 collective-permute-start
  16.9 127.2 %copy-start.2 = (f32[1,2048]{1,0:T(1,128)}, f32[1,2048]{1,0:T(1,128)S(1)}, u32[]{:S(2)}) copy-start(f32[1,2048]{1,0:T(1,128)S(1)} %get-tuple-element.162) | copy-start | bytes 24580
  16.9 127.2 %copy-start.4 = (f32[1,2048]{1,0:T(1,128)}, f32[1,2048]{1,0:T(1,128)S(1)}, u32[]{:S(2)}) copy-start(f32[1,2048]{1,0:T(1,128)S(1)} %get-tuple-element.163) | copy-start | bytes 24580
  16.9 127.2 %copy-start.6 = (f32[1,2048]{1,0:T(1,128)}, f32[1,2048]{1,0:T(1,128)S(1)}, u32[]{:S(2)}) copy-start(f32[1,2048]{1,0:T(1,128)S(1)} %get-tuple-element.164) | copy-start | bytes 24580
  17.0 127.2 %copy-start.8 = (f32[1,2048]{1,0:T(1,128)}, f32[1,2048]{1,0:T(1,128)S(1)}, u32[]{:S(2)}) copy-start(f32[1,2048]{1,0:T(1,128)S(1)} %get-tuple-element.165) | copy-start | bytes 24580
  17.0 127.2 %copy-start.10 = (f32[1,2048]{1,0:T(1,128)}, f32[1,2048]{1,0:T(1,128)S(1)}, u32[]{:S(2)}) copy-start(f32[1,2048]{1,0:T(1,128)S(1)} %get-tuple-element.166) | copy-start | bytes 24580
  17.0 127.2 %copy-start.12 = (f32[1,2048]{1,0:T(1,128)}, f32[1,2048]{1,0:T(1,128)S(1)}, u32[]{:S(2)}) copy-start(f32[1,2048]{1,0:T(1,128)S(1)} %get-tuple-element.167) | copy-start | bytes 24580
  17.0 127.2 %copy-start.14 = (f32[1,2048]{1,0:T(1,128)}, f32[1,2048]{1,0:T(1,128)S(1)}, u32[]{:S(2)}) copy-start(f32[1,2048]{1,0:T(1,128)S(1)} %get-tuple-element.168) | copy-start | bytes 24580
  170.5 3.8 copy-start.16
  214.8 3.8 copy-start.16
  259.1 3.8 copy-start.16
  303.5 3.8 copy-start.16
  346.4 202.0 %reduce-scatter.9.cloned.1.call-start = ((), (), s32[]{:S(2)}) async-start(), calls=%async_computation.5 | async-start | bytes 8912896
  371.3 1.0 copy-start.1
  372.5 84.8 %copy-start.3 = (f32[1,2048]{1,0:T(1,128)S(1)}, f32[1,2048]{1,0:T(1,128)}, u32[]{:S(2)}) copy-start(f32[1,2048]{1,0:T(1,128)} %copy-done.2) | copy-start | bytes 24580
  372.5 84.8 %copy-start.5 = (f32[1,2048]{1,0:T(1,128)S(1)}, f32[1,2048]{1,0:T(1,128)}, u32[]{:S(2)}) copy-start(f32[1,2048]{1,0:T(1,128)} %copy-done.4) | copy-start | bytes 24580
  372.6 84.8 %copy-start.7 = (f32[1,2048]{1,0:T(1,128)S(1)}, f32[1,2048]{1,0:T(1,128)}, u32[]{:S(2)}) copy-start(f32[1,2048]{1,0:T(1,128)} %copy-done.6) | copy-start | bytes 24580
  372.6 84.7 %copy-start.9 = (f32[1,2048]{1,0:T(1,128)S(1)}, f32[1,2048]{1,0:T(1,128)}, u32[]{:S(2)}) copy-start(f32[1,2048]{1,0:T(1,128)} %copy-done.8) | copy-start | bytes 24580
  372.6 84.7 %copy-start.11 = (f32[1,2048]{1,0:T(1,128)S(1)}, f32[1,2048]{1,0:T(1,128)}, u32[]{:S(2)}) copy-start(f32[1,2048]{1,0:T(1,128)} %copy-done.10) | copy-start | bytes 24580
  372.6 84.7 %copy-start.13 = (f32[1,2048]{1,0:T(1,128)S(1)}, f32[1,2048]{1,0:T(1,128)}, u32[]{:S(2)}) copy-start(f32[1,2048]{1,0:T(1,128)} %copy-done.12) | copy-start | bytes 24580
  372.6 84.7 %copy-start.15 = (f32[1,2048]{1,0:T(1,128)S(1)}, f32[1,2048]{1,0:T(1,128)}, u32[]{:S(2)}) copy-start(f32[1,2048]{1,0:T(1,128)} %copy-done.14) | copy-start | bytes 24580
  373.0 4.9 collective-permute-start.3
  373.7 4.3 collective-permute-start.2
Sparse Core Ops, SparseCore 0:
  10.4 68.3 all-gather.4
  81.1 63.0 all-gather.6
  346.6 99.6 reduce-scatter.6
  448.7 99.6 reduce-scatter.8
where the time goes:
time: 560 us; the launch traced here: 558 us
  waiting for transfers between devices  210 us (38%)
  matrix products  125 us (22%)
  local copies, waits for them, and re-layouts  116 us (21%)
  blocking collectives  78.2 us (14%)
  between operations  14.1 us (3%)
  other arithmetic  5.7 us (1%)
  starting transfers between devices  5.66 us (1%)
    unnamed x6, waiting for transfers between devices  86.6 us
    psum x1, blocking collectives, on_device(): filter_gradient = lax.psum(jnp.stack(filter_rows, 0), ('dp', 'seq'))  78.2 us
    all_gather x1, waiting for transfers between devices, on_device(): lax.all_gather(local_k, 'seq', axis=0, tiled=True)  65.4 us
    unnamed x46, local copies, waits for them, and re-layouts  62.6 us
    all_gather x1, waiting for transfers between devices, on_device(): lax.all_gather(local_v, 'seq', axis=0, tiled=True)  57.9 us
    dot_general x4, matrix products, forward_group(): jnp.einsum('htu,thd->uhd', dscore, q_part, preferred_element_type=jnp.flo...  38 us
    dot_general x4, matrix products, forward_group(): jnp.einsum('htu,uhd->thd', dscore, k_part, preferred_element_type=jnp.flo...  34.2 us
    dynamic_slice x20, local copies, waits for them, and re-layouts, columns(): lax.dynamic_slice_in_dim(matrix, group_index * group_width, group_width, 1)  27.5 us
  transfers between devices with their start and end apart: 8, of which 3 were waited for; matrix products, arithmetic and copies ran while one was open for 7% of the time, Pallas kernels for 0%

commit v1 on v0

v1 whole, which is shorter than its diff:
```python
import math

import jax
import jax.numpy as jnp
import numpy as np
from jax import lax
from jax.sharding import Mesh
from jax.sharding import PartitionSpec as P

HD = 128
TAPS = 7
GROUP_HEADS = 2

SEQ = ("sc", "core")


def padded(value, width):
    peers = lax.axis_size("sc") * lax.axis_size("core")
    length = value.shape[0]
    up = [(i, (i + 1) % peers) for i in range(peers)]
    down = [(j, i) for i, j in up]
    before = lax.ppermute(value[length - width :], SEQ, up)
    after = lax.ppermute(value[:width], SEQ, down)
    return jnp.concatenate([before, value, after], axis=0)


def to_chip_rows(value):
    rows, channels = value.shape
    split = value.reshape(rows, 2, channels // 2)
    return lax.all_to_all(split, "core", 1, 0, tiled=True).reshape(2 * rows, channels // 2)


def from_chip_rows(value):
    rows2, half = value.shape
    split = value.reshape(2, rows2 // 2, 1, half)
    out = lax.all_to_all(split, "core", 0, 2, tiled=True)
    return out.reshape(rows2 // 2, 2 * half)


def on_device(queries, key_states, value_states, cotangent, filter_taps):
    tok_rows = queries.shape[1]
    channels = queries.shape[2]
    chips = lax.axis_size("sc")
    seq_total = tok_rows * chips * 2
    chip_rows = 2 * tok_rows
    half_channels = channels // 2
    head_count = half_channels // HD
    group_width = GROUP_HEADS * HD
    group_count = head_count // GROUP_HEADS
    score_scale = HD ** (-0.5)
    half_width = (TAPS - 1) // 2
    local_q = queries[0]
    local_k = key_states[0]
    local_v = value_states[0]
    local_g = cotangent[0]
    grad_pad = padded(local_g, half_width)
    grad_sum = jnp.zeros((tok_rows, channels), jnp.float32)
    for tap_index in range(TAPS):
        start_row = 2 * half_width - tap_index
        grad_sum = grad_sum + filter_taps[tap_index] * grad_pad[
            start_row : start_row + tok_rows
        ].astype(jnp.float32)
    grad_attn = grad_sum.astype(jnp.bfloat16)

    chip_q = to_chip_rows(local_q)
    chip_k = to_chip_rows(local_k)
    chip_v = to_chip_rows(local_v)
    chip_d = to_chip_rows(grad_attn)

    chip_index = lax.axis_index("sc")
    query_pos = chip_index * chip_rows + jnp.arange(chip_rows, dtype=jnp.int32)
    key_pos = jnp.arange(seq_total, dtype=jnp.int32)
    visible = query_pos[:, None] >= key_pos[None, :]

    attended_parts, grad_q_parts, key_parts, value_parts = [], [], [], []
    for group_index in range(group_count):
        cols = slice(group_index * group_width, (group_index + 1) * group_width)
        k_all = lax.all_gather(chip_k[:, cols], "sc", axis=0, tiled=True)
        v_all = lax.all_gather(chip_v[:, cols], "sc", axis=0, tiled=True)
        q_part = chip_q[:, cols].reshape(chip_rows, GROUP_HEADS, HD)
        d_part = chip_d[:, cols].reshape(chip_rows, GROUP_HEADS, HD)
        k_part = k_all.reshape(seq_total, GROUP_HEADS, HD)
        v_part = v_all.reshape(seq_total, GROUP_HEADS, HD)
        scores = (
            jnp.einsum("thd,uhd->htu", q_part, k_part, preferred_element_type=jnp.float32)
            * score_scale
        )
        row_top = jnp.max(jnp.where(visible, scores, -jnp.inf), -1, keepdims=True)
        raw = jnp.where(visible, jnp.exp(scores - row_top), 0.0)
        row_total = jnp.sum(raw, -1, keepdims=True)
        probs = raw / row_total
        probs_low = probs.astype(jnp.bfloat16)
        attended = jnp.einsum("htu,uhd->thd", probs_low, v_part, preferred_element_type=jnp.float32)
        attended_parts.append(attended.astype(jnp.bfloat16).reshape(chip_rows, group_width))
        dprob = jnp.einsum("thd,uhd->htu", d_part, v_part, preferred_element_type=jnp.float32)
        row_delta = jnp.sum(probs * dprob, -1, keepdims=True)
        dscore = (probs * (dprob - row_delta) * score_scale).astype(jnp.bfloat16)
        grad_q = jnp.einsum("htu,uhd->thd", dscore, k_part, preferred_element_type=jnp.float32)
        grad_q_parts.append(grad_q.astype(jnp.bfloat16).reshape(chip_rows, group_width))
        key_term = jnp.einsum("htu,thd->uhd", dscore, q_part, preferred_element_type=jnp.float32)
        value_term = jnp.einsum("htu,thd->uhd", probs_low, d_part, preferred_element_type=jnp.float32)
        key_parts.append(
            lax.psum_scatter(
                key_term.astype(jnp.bfloat16).reshape(seq_total, group_width),
                "sc", scatter_dimension=0, tiled=True,
            )
        )
        value_parts.append(
            lax.psum_scatter(
                value_term.astype(jnp.bfloat16).reshape(seq_total, group_width),
                "sc", scatter_dimension=0, tiled=True,
            )
        )

    attn_out = from_chip_rows(jnp.concatenate(attended_parts, axis=1))
    grad_queries = from_chip_rows(jnp.concatenate(grad_q_parts, axis=1))
    grad_keys = from_chip_rows(jnp.concatenate(key_parts, axis=1))
    grad_values = from_chip_rows(jnp.concatenate(value_parts, axis=1))

    out_pad = padded(attn_out, half_width)
    conv_sum = jnp.zeros((tok_rows, channels), jnp.float32)
    filter_rows = []
    local_gf = local_g.astype(jnp.float32)
    for tap_index in range(TAPS):
        moved = out_pad[tap_index : tap_index + tok_rows].astype(jnp.float32)
        conv_sum = conv_sum + filter_taps[tap_index] * moved
        filter_rows.append(jnp.sum(moved * local_gf, 0))
    filter_gradient = lax.psum(jnp.stack(filter_rows, 0), ("dp", "sc", "core"))
    conv_output = conv_sum.astype(jnp.bfloat16)
    return (
        conv_output[None],
        grad_queries[None],
        grad_keys[None],
        grad_values[None],
        filter_gradient,
    )


def solution(mesh):
    devices = np.asarray(mesh.devices)
    dp_size, seq_size = devices.shape
    split_mesh = Mesh(devices.reshape(dp_size, seq_size // 2, 2), ("dp", "sc", "core"))
    block = P("dp", SEQ, None)
    in_specs = (block, block, block, block, P())
    out_specs = (block, block, block, block, P())
    return jax.shard_map(
        on_device, mesh=split_mesh, in_specs=in_specs, out_specs=out_specs, check_vma=False
    )
```

time: 560 us -> 750 us (1.34)
  waiting for transfers between devices: 210 us -> 404 us
  local copies, waits for them, and re-layouts: 116 us -> 38.6 us
  blocking collectives: 78.2 us -> 110 us
  starting transfers between devices: 5.66 us -> 20.4 us
  other arithmetic: 5.7 us -> 17.8 us
  matrix products: 125 us -> 136 us
    reduce_scatter x0 -> x8, waiting for transfers between devices: none -> 154 us  [the longest x4 154 us: on_device(): lax.psum_scatter(value_term.astype(jnp.bfloat16).reshape(seq_total, group...]
    all_gather x2 -> x8, waiting for transfers between devices: 123 us -> 217 us  [the longest x4 159 us: on_device(): v_all = lax.all_gather(chip_v[:, cols], 'sc', axis=0, tiled=True)]
    unnamed x6 -> x16, waiting for transfers between devices: 86.6 us -> 3.14 us
    unnamed x46 -> x65, local copies, waits for them, and re-layouts: 62.6 us -> 7.49 us
    dynamic_slice x24 -> x0, local copies, waits for them, and re-layouts: 29.9 us -> none  [the longest x20 27.5 us: columns(): lax.dynamic_slice_in_dim(matrix, group_index * group_width, group_width, 1)]
    ppermute x4, waiting for transfers between devices: 0.01 us -> 29 us  [the longest x2 28 us: padded(): after = lax.ppermute(value[:width], SEQ, down)]
    all_to_all x0 -> x5, blocking collectives: none -> 28.3 us  [the longest x3 15.1 us: to_chip_rows(): lax.all_to_all(split, 'core', 1, 0, tiled=True)]
    dynamic_update_slice x8 -> x0, local copies, waits for them, and re-layouts: 18.7 us -> none  [on_device(): attended, grad_q, key_term, value_term = lax.map(forward_group, group_ids)]
  transfers between devices with their start and end apart: 8 -> 23, of which waited for: 3 -> 15; matrix products, arithmetic and copies ran while one was open for 7% -> 25% of each run, Pallas kernels for 0% -> 0%
where the time goes in v1:
time: 750 us; the launch traced here: 741 us
  waiting for transfers between devices  404 us (54%)
  matrix products  136 us (18%)
  blocking collectives  110 us (15%)
  local copies, waits for them, and re-layouts  38.6 us (5%)
  starting transfers between devices  20.4 us (3%)
  other arithmetic  17.8 us (2%)
  between operations  15.1 us (2%)
    all_gather x4, waiting for transfers between devices, on_device(): v_all = lax.all_gather(chip_v[:, cols], 'sc', axis=0, tiled=True)  159 us
    reduce_scatter x4, waiting for transfers between devices, on_device(): lax.psum_scatter(value_term.astype(jnp.bfloat16).reshape(seq_total, group...  154 us
    psum x1, blocking collectives, on_device(): filter_gradient = lax.psum(jnp.stack(filter_rows, 0), ('dp', 'sc', 'core'))  81.5 us
    all_gather x4, waiting for transfers between devices, on_device(): k_all = lax.all_gather(chip_k[:, cols], 'sc', axis=0, tiled=True)  58.1 us
    dot_general x4, matrix products, on_device(): jnp.einsum('htu,thd->uhd', dscore, q_part, preferred_element_type=jnp.flo...  38.7 us
    dot_general x4, matrix products, on_device(): jnp.einsum('htu,uhd->thd', dscore, k_part, preferred_element_type=jnp.flo...  32.3 us
    ppermute x2, waiting for transfers between devices, padded(): after = lax.ppermute(value[:width], SEQ, down)  28 us
    sub x4, matrix products, on_device(): raw = jnp.where(visible, jnp.exp(scores - row_top), 0.0)  24.9 us
  transfers between devices with their start and end apart: 23, of which 15 were waited for; matrix products, arithmetic and copies ran while one was open for 25% of the time, Pallas kernels for 0%

profile of v1, /device:TPU:1, one launch (start us, length us, event | category | flops | bytes accessed | tf_op | source)
XLA Modules:
  0.0 740.9 jit_solution(332086236696625652)
XLA Ops:
  8.6 7.2 all_to_all.120
  17.2 4.2 all_to_all.121
  26.6 3.9 all-to-all-start
  36.2 20.8 %collective-permute-done.2 = bf16[3,2048]{0,1:T(8,128)(2,1)S(1)} collective-permute-done((bf16[3,2048]{0,1:T(8,128)(2,1)}, bf16[3,2048]{0,1:T(8,128)(2,1)S(1)}, u32[]{:S(2)}, u32[]{:S(2)}) %collective-permute-start.2) | collective-permute-done | bytes 12320 | tf_op jit(solution)/shard_map/ppermute | solution.py:23
  58.1 5.9 fusion.115
  64.0 3.8 all_to_all.122
  71.0 34.5 %all-gather.15.cloned.1.call-done = bf16[2048,256]{1,0:T(8,128)(2,1)} async-done(((bf16[256,256]{1,0:T(8,128)(2,1)}), bf16[2048,256]{1,0:T(8,128)(2,1)}) %all-gather.15.cloned.1.call-update) | async-done | bytes 1048592 | tf_op jit(solution)/shard_map/all_gather | solution.py:79
  107.0 3.6 fusion.183
  110.6 5.9 fusion.180
  116.5 9.7 %convolution_convert_fusion.2 = bf16[2,2048,128]{1,2,0:T(8,128)(2,1)} fusion(bf16[256,2,128]{0,2,1:T(8,128)(2,1)} %bitcast.232, f32[2,256,2048]{2,1,0:T(8,128)} %fusion.183, f32[2,256,2048]{2,1,0:T(8,128)} %get-tuple-element.66, f32[2,256]{1,0:T(2,128)} %get-tuple-element.65), kind=kOutput, calls=%fused_computation.45 | convolution fusion | flops 276302336 | bytes 9570304 | tf_op jit(solution)/shard_map/htu,thd->uhd/dot_general | solution.py:100
  128.2 20.3 %all-gather.17.cloned.1.call-done = bf16[2048,256]{1,0:T(8,128)(2,1)} async-done(((bf16[256,256]{1,0:T(8,128)(2,1)}), bf16[2048,256]{1,0:T(8,128)(2,1)}) %all-gather.17.cloned.1.call-update) | async-done | bytes 1048592 | tf_op jit(solution)/shard_map/all_gather | solution.py:78
  150.8 40.5 %all-gather.19.cloned.1.call-done = bf16[2048,256]{1,0:T(8,128)(2,1)} async-done(((bf16[256,256]{1,0:T(8,128)(2,1)}), bf16[2048,256]{1,0:T(8,128)(2,1)}) %all-gather.19.cloned.1.call-update) | async-done | bytes 1048592 | tf_op jit(solution)/shard_map/all_gather | solution.py:79
  192.8 3.6 fusion.184
  196.4 6.5 fusion.179
  203.0 9.7 %convolution_convert_fusion.1 = bf16[2,2048,128]{1,2,0:T(8,128)(2,1)} fusion(bf16[256,2,128]{0,2,1:T(8,128)(2,1)} %bitcast.236, f32[2,256,2048]{2,1,0:T(8,128)} %fusion.184, f32[2,256,2048]{2,1,0:T(8,128)} %get-tuple-element.64, f32[2,256]{1,0:T(2,128)} %get-tuple-element.63), kind=kOutput, calls=%fused_computation.44 | convolution fusion | flops 276302336 | bytes 9570304 | tf_op jit(solution)/shard_map/htu,thd->uhd/dot_general | solution.py:100
  214.5 19.3 %all-gather.21.cloned.1.call-done = bf16[2048,256]{1,0:T(8,128)(2,1)} async-done(((bf16[256,256]{1,0:T(8,128)(2,1)}), bf16[2048,256]{1,0:T(8,128)(2,1)}) %all-gather.21.cloned.1.call-update) | async-done | bytes 1048592 | tf_op jit(solution)/shard_map/all_gather | solution.py:78
  236.0 41.4 %all-gather.23.cloned.1.call-done = bf16[2048,256]{1,0:T(8,128)(2,1)} async-done(((bf16[256,256]{1,0:T(8,128)(2,1)}), bf16[2048,256]{1,0:T(8,128)(2,1)}) %all-gather.23.cloned.1.call-update) | async-done | bytes 1048592 | tf_op jit(solution)/shard_map/all_gather | solution.py:79
  279.7 3.9 fusion.185
  283.6 6.5 fusion.178
  290.1 9.7 %convolution_convert_fusion = bf16[2,2048,128]{1,2,0:T(8,128)(2,1)} fusion(bf16[256,2,128]{0,2,1:T(8,128)(2,1)} %bitcast.238, f32[2,256,2048]{2,1,0:T(8,128)} %fusion.185, f32[2,256,2048]{2,1,0:T(8,128)} %get-tuple-element.62, f32[2,256]{1,0:T(2,128)} %get-tuple-element.61), kind=kOutput, calls=%fused_computation.43 | convolution fusion | flops 276302336 | bytes 9570304 | tf_op jit(solution)/shard_map/htu,thd->uhd/dot_general | solution.py:100
  301.0 18.5 %all-gather.9.cloned.1.call-done = bf16[2048,256]{1,0:T(8,128)(2,1)} async-done(((bf16[256,256]{1,0:T(8,128)(2,1)}), bf16[2048,256]{1,0:T(8,128)(2,1)}) %all-gather.9.cloned.1.call-update) | async-done | bytes 1048592 | tf_op jit(solution)/shard_map/all_gather | solution.py:78
  321.8 42.1 %all-gather.11.cloned.1.call-done = bf16[2048,256]{1,0:T(8,128)(2,1)} async-done(((bf16[256,256]{1,0:T(8,128)(2,1)}), bf16[2048,256]{1,0:T(8,128)(2,1)}) %all-gather.11.cloned.1.call-update) | async-done | bytes 1048592 | tf_op jit(solution)/shard_map/all_gather | solution.py:79
  366.2 3.9 fusion.182
  370.1 6.0 fusion.181
  376.1 9.6 %convolution_convert_fusion.3 = bf16[2,2048,128]{1,2,0:T(8,128)(2,1)} fusion(bf16[256,2,128]{0,2,1:T(8,128)(2,1)S(1)} %bitcast.234, f32[2,256,2048]{2,1,0:T(8,128)} %fusion.182, f32[2,256,2048]{2,1,0:T(8,128)} %get-tuple-element.68, f32[2,256]{1,0:T(2,128)S(1)} %get-tuple-element.67), kind=kOutput, calls=%fused_computation.46 | convolution fusion | flops 276302336 | bytes 9570304 | tf_op jit(solution)/shard_map/htu,thd->uhd/dot_general | solution.py:100
  385.8 3.8 convolution_convert_fusion.6
  389.7 3.7 convolution_convert_fusion.5
  393.5 3.0 fusion.101
  396.7 8.2 %fusion.91 = bf16[256,2,128]{2,0,1:T(8,128)(2,1)S(1)} fusion(bf16[2048,2,128]{0,2,1:T(8,128)(2,1)} %bitcast.215, f32[2,256,2048]{2,1,0:T(8,128)} %fusion.183, f32[2,256,2048]{2,1,0:T(8,128)} %get-tuple-element.66, f32[2,256]{1,0:T(2,128)S(1)} %copy-done.23), kind=kOutput, calls=%fused_computation.111 | convolution fusion | flops 275843584 | bytes 9570304 | tf_op jit(solution)/shard_map/htu,uhd->thd/dot_general | solution.py:98
  405.2 3.0 fusion.102
  408.4 3.8 convolution_convert_fusion.4
  412.5 7.9 %fusion.94 = bf16[256,2,128]{2,0,1:T(8,128)(2,1)S(1)} fusion(bf16[2048,2,128]{0,2,1:T(8,128)(2,1)S(1)} %bitcast.217, f32[2,256,2048]{2,1,0:T(8,128)} %fusion.184, f32[2,256,2048]{2,1,0:T(8,128)} %get-tuple-element.64, f32[2,256]{1,0:T(2,128)S(1)} %copy-done.24), kind=kOutput, calls=%fused_computation.112 | convolution fusion | flops 275843584 | bytes 9570304 | tf_op jit(solution)/shard_map/htu,uhd->thd/dot_general | solution.py:98
  420.7 3.0 fusion.103
  424.0 4.0 convolution_convert_fusion.7
  429.2 8.1 %fusion.97 = bf16[256,2,128]{2,0,1:T(8,128)(2,1)S(1)} fusion(bf16[2048,2,128]{0,2,1:T(8,128)(2,1)S(1)} %bitcast.219, f32[2,256,2048]{2,1,0:T(8,128)} %fusion.185, f32[2,256,2048]{2,1,0:T(8,128)} %get-tuple-element.62, f32[2,256]{1,0:T(2,128)} %get-tuple-element.61), kind=kOutput, calls=%fused_computation.113 | convolution fusion | flops 275843584 | bytes 9570304 | tf_op jit(solution)/shard_map/htu,uhd->thd/dot_general | solution.py:98
  437.8 8.0 %fusion.88 = bf16[256,2,128]{2,0,1:T(8,128)(2,1)S(1)} fusion(bf16[2048,2,128]{0,2,1:T(8,128)(2,1)S(1)} %bitcast.221, f32[2,256,2048]{2,1,0:T(8,128)} %fusion.182, f32[2,256,2048]{2,1,0:T(8,128)} %get-tuple-element.68, f32[2,256]{1,0:T(2,128)} %copy-done.26), kind=kOutput, calls=%fused_computation.110 | convolution fusion | flops 275843584 | bytes 9570304 | tf_op jit(solution)/shard_map/htu,uhd->thd/dot_general | solution.py:98
  446.9 8.7 %all-to-all-start.3 = ((bf16[2,128,1,1024]{3,1,2,0:T(8,128)(2,1)}), bf16[2,128,1,1024]{3,1,2,0:T(8,128)(2,1)S(1)}, u32[]{:S(2)}, u32[]{:S(2)}) async-start(bf16[2,128,1,1024]{3,1,2,0:T(8,128)(2,1)} %maximum_bitcast_fusion), calls=%async_computation.3 | async-start | bytes 1048576 | tf_op jit(solution)/shard_map/all_to_all | solution.py:36
  457.0 3.9 all-to-all-start.5
  464.4 7.2 collective-permute-done.1
  471.6 3.8 fusion.139
  476.3 3.4 fusion.121
  479.8 81.5 %psum.7 = f32[7,2048]{1,0:T(8,128)} all-reduce(f32[7,2048]{1,0:T(8,128)S(1)} %stack.31), channel_id=1, replica_groups=mesh['dp'=16,'sc'=8,'core'=2] {'dp','sc','core'}, use_global_device_ids=true, to_apply=%region_27.28 | all-reduce | flops 14336 | bytes 114688 | tf_op jit(solution)/shard_map/psum | solution.py:128
  562.7 24.0 %reduce-scatter.19.cloned.1.call-done = bf16[256,256]{0,1:T(8,128)(2,1)} async-done(((bf16[2048,256]{0,1:T(8,128)(2,1)}), bf16[256,256]{0,1:T(8,128)(2,1)}) %reduce-scatter.19.cloned.1.call-update) | async-done | bytes 131088 | tf_op jit(solution)/shard_map/reduce_scatter | solution.py:109
  586.6 43.4 %reduce-scatter.21.cloned.1.call-done = bf16[256,256]{0,1:T(8,128)(2,1)} async-done(((bf16[2048,256]{0,1:T(8,128)(2,1)}), bf16[256,256]{0,1:T(8,128)(2,1)}) %reduce-scatter.21.cloned.1.call-update) | async-done | bytes 131088 | tf_op jit(solution)/shard_map/reduce_scatter | solution.py:109
  630.0 43.4 %reduce-scatter.23.cloned.1.call-done = bf16[256,256]{0,1:T(8,128)(2,1)} async-done(((bf16[2048,256]{0,1:T(8,128)(2,1)}), bf16[256,256]{0,1:T(8,128)(2,1)}) %reduce-scatter.23.cloned.1.call-update) | async-done | bytes 131088 | tf_op jit(solution)/shard_map/reduce_scatter | solution.py:109
  673.4 43.4 %reduce-scatter.17.cloned.1.call-done = bf16[256,256]{0,1:T(8,128)(2,1)} async-done(((bf16[2048,256]{0,1:T(8,128)(2,1)}), bf16[256,256]{0,1:T(8,128)(2,1)}) %reduce-scatter.17.cloned.1.call-update) | async-done | bytes 131088 | tf_op jit(solution)/shard_map/reduce_scatter | solution.py:109
  718.2 9.0 %all_to_all.123 = bf16[2,128,1,1024]{3,1,2,0:T(8,128)(2,1)S(1)} all-to-all(bf16[2,128,1,1024]{3,1,2,0:T(8,128)(2,1)S(1)} %bitcast.199), channel_id=1, replica_groups=mesh['dp'=16,'sc'=8,'core'=2] {'core'}, dimensions={0} | all-to-all | bytes 1048576 | tf_op jit(solution)/shard_map/all_to_all | solution.py:36
  728.5 4.1 all_to_all.124
  (171 shorter events, 52.8 us)
Async XLA Ops:
  7.2 9.7 %copy-start.6 = (bf16[1,128,2048]{2,1,0:T(8,128)(2,1)S(1)}, bf16[1,128,2048]{2,1,0:T(8,128)(2,1)}, u32[]{:S(2)}) copy-start(bf16[1,128,2048]{2,1,0:T(8,128)(2,1)} %param.7) | copy-start | bytes 1572868
  7.2 62.3 %all-gather.13.cloned.1.call-start = ((), (), s32[]{:S(2)}) async-start(), calls=%async_computation.18 | async-start | bytes 1179648 | tf_op jit(solution)/shard_map/all_gather | solution.py:78
  8.6 17.0 %copy-start.7 = (bf16[1,128,2048]{2,1,0:T(8,128)(2,1)S(1)}, bf16[1,128,2048]{2,1,0:T(8,128)(2,1)}, u32[]{:S(2)}) copy-start(bf16[1,128,2048]{2,1,0:T(8,128)(2,1)} %param.5) | copy-start | bytes 1572868
  16.0 14.5 %copy-start.8 = (bf16[1,128,2048]{2,1,0:T(8,128)(2,1)S(1)}, bf16[1,128,2048]{2,1,0:T(8,128)(2,1)}, u32[]{:S(2)}) copy-start(bf16[1,128,2048]{2,1,0:T(8,128)(2,1)} %param.8) | copy-start | bytes 1572868
  16.8 88.7 %all-gather.15.cloned.1.call-start = ((), (), s32[]{:S(2)}) async-start(), calls=%async_computation.19 | async-start | bytes 1179648 | tf_op jit(solution)/shard_map/all_gather | solution.py:79
  21.3 12.2 %copy-start.21 = (f32[7,2048]{1,0:T(8,128)S(1)}, f32[7,2048]{1,0:T(8,128)}, u32[]{:S(2)}) copy-start(f32[7,2048]{1,0:T(8,128)} %param.9) | copy-start | bytes 172036
  22.4 126.2 %all-gather.17.cloned.1.call-start = ((), (), s32[]{:S(2)}) async-start(), calls=%async_computation.20 | async-start | bytes 1179648 | tf_op jit(solution)/shard_map/all_gather | solution.py:78
  23.1 168.2 %all-gather.19.cloned.1.call-start = ((), (), s32[]{:S(2)}) async-start(), calls=%async_computation.21 | async-start | bytes 1179648 | tf_op jit(solution)/shard_map/all_gather | solution.py:79
  23.7 210.1 %all-gather.21.cloned.1.call-start = ((), (), s32[]{:S(2)}) async-start(), calls=%async_computation.22 | async-start | bytes 1179648 | tf_op jit(solution)/shard_map/all_gather | solution.py:78
  24.3 253.1 %all-gather.23.cloned.1.call-start = ((), (), s32[]{:S(2)}) async-start(), calls=%async_computation.23 | async-start | bytes 1179648 | tf_op jit(solution)/shard_map/all_gather | solution.py:79
  24.8 294.7 %all-gather.9.cloned.1.call-start = ((), (), s32[]{:S(2)}) async-start(), calls=%async_computation.16 | async-start | bytes 1179648 | tf_op jit(solution)/shard_map/all_gather | solution.py:78
  26.6 8.0 %all-to-all-start = ((bf16[128,2,1024]{0,2,1:T(8,128)(2,1)}), bf16[128,2,1024]{0,2,1:T(8,128)(2,1)S(1)}, u32[]{:S(2)}, u32[]{:S(2)}) async-start(bf16[128,2,1024]{0,2,1:T(8,128)(2,1)} %bitcast.1), calls=%async_computation | async-start | bytes 1048576 | tf_op jit(solution)/shard_map/all_to_all | solution.py:30
  30.5 333.5 %all-gather.11.cloned.1.call-start = ((), (), s32[]{:S(2)}) async-start(), calls=%async_computation.17 | async-start | bytes 1179648 | tf_op jit(solution)/shard_map/all_gather | solution.py:79
  31.7 25.3 %collective-permute-start.2 = (bf16[3,2048]{0,1:T(8,128)(2,1)}, bf16[3,2048]{0,1:T(8,128)(2,1)S(1)}, u32[]{:S(2)}, u32[]{:S(2)}) collective-permute-start(bf16[3,2048]{0,1:T(8,128)(2,1)} %get-tuple-element.38), channel_id=1, source_target_pairs={{1,0},{2,1},{3,2},{4,3},{5,4},{6,5},{7,6},{8,7},{9,8},{10,9},{11,1... | collective-permute-start | bytes 36872 | tf_op jit(solution)/shard_map/ppermute | solution.py:23
  31.8 26.3 %collective-permute-start.3 = (bf16[3,2048]{0,1:T(8,128)(2,1)S(1)}, bf16[3,2048]{0,1:T(8,128)(2,1)}, u32[]{:S(2)}, u32[]{:S(2)}) collective-permute-start(bf16[3,2048]{0,1:T(8,128)(2,1)S(1)} %get-tuple-element.39), channel_id=1, source_target_pairs={{0,1},{1,2},{2,3},{3,4},{4,5},{5,6},{6,7},{7,8},{8,9},{9,10},{10,1... | collective-permute-start | bytes 36872 | tf_op jit(solution)/shard_map/ppermute | solution.py:22
  33.5 527.8 %reduce-scatter.11.cloned.1.call-start = ((), (), s32[]{:S(2)}) async-start(), calls=%async_computation.25 | async-start | bytes 1179648 | tf_op jit(solution)/shard_map/reduce_scatter | solution.py:103
  71.0 45.5 %copy-start.2 = (bf16[2048,256]{0,1:T(8,128)(2,1)}, bf16[2048,256]{0,1:T(8,128)(2,1)S(1)}, u32[]{:S(2)}) copy-start(bf16[2048,256]{0,1:T(8,128)(2,1)S(1)} %copy.289) | copy-start | bytes 3145732
  116.5 10.2 %copy-start.9 = (bf16[256,256]{1,0:T(8,128)(2,1)S(1)}, bf16[256,256]{1,0:T(8,128)(2,1)}, u32[]{:S(2)}) copy-start(bf16[256,256]{1,0:T(8,128)(2,1)} %get-tuple-element.48) | copy-start | bytes 393220
  116.5 11.0 %copy-start.10 = (bf16[256,256]{1,0:T(8,128)(2,1)S(1)}, bf16[256,256]{1,0:T(8,128)(2,1)}, u32[]{:S(2)}) copy-start(bf16[256,256]{1,0:T(8,128)(2,1)} %get-tuple-element.36) | copy-start | bytes 393220
  126.1 435.1 %reduce-scatter.13.cloned.1.call-start = ((), (), s32[]{:S(2)}) async-start(), calls=%async_computation.26 | async-start | bytes 1179648 | tf_op jit(solution)/shard_map/reduce_scatter | solution.py:103
  212.7 348.6 %reduce-scatter.15.cloned.1.call-start = ((), (), s32[]{:S(2)}) async-start(), calls=%async_computation.27 | async-start | bytes 1179648 | tf_op jit(solution)/shard_map/reduce_scatter | solution.py:103
  299.9 261.4 %reduce-scatter.9.cloned.1.call-start = ((), (), s32[]{:S(2)}) async-start(), calls=%async_computation.24 | async-start | bytes 1179648 | tf_op jit(solution)/shard_map/reduce_scatter | solution.py:103
  301.0 69.1 %copy-start.13 = (bf16[256,256]{0,1:T(8,128)(2,1)}, bf16[256,256]{0,1:T(8,128)(2,1)S(1)}, u32[]{:S(2)}) copy-start(bf16[256,256]{0,1:T(8,128)(2,1)S(1)} %copy.319) | copy-start | bytes 393220
  321.8 48.3 %copy-start.15 = (bf16[256,256]{0,1:T(8,128)(2,1)S(1)}, bf16[256,256]{0,1:T(8,128)(2,1)}, u32[]{:S(2)}) copy-start(bf16[256,256]{0,1:T(8,128)(2,1)} %copy.277) | copy-start | bytes 393220
  376.1 9.6 %copy-start.26 = (f32[2,256]{1,0:T(2,128)}, f32[2,256]{1,0:T(2,128)S(1)}, u32[]{:S(2)}) copy-start(f32[2,256]{1,0:T(2,128)S(1)} %get-tuple-element.67) | copy-start | bytes 6148
  376.1 9.7 %copy-start.11 = (bf16[256,256]{0,1:T(8,128)(2,1)S(1)}, bf16[256,256]{0,1:T(8,128)(2,1)}, u32[]{:S(2)}) copy-start(bf16[256,256]{0,1:T(8,128)(2,1)} %copy.324) | copy-start | bytes 393220
  376.1 9.7 %copy-start.23 = (f32[2,256]{1,0:T(2,128)S(1)}, f32[2,256]{1,0:T(2,128)}, u32[]{:S(2)}) copy-start(f32[2,256]{1,0:T(2,128)} %get-tuple-element.65) | copy-start | bytes 6148
  385.7 3.9 copy-start.12
  385.7 3.9 copy-start.24
  385.7 200.9 %reduce-scatter.19.cloned.1.call-start = ((), (), s32[]{:S(2)}) async-start(), calls=%async_computation.29 | async-start | bytes 1179648 | tf_op jit(solution)/shard_map/reduce_scatter | solution.py:109
  389.6 240.4 %reduce-scatter.21.cloned.1.call-start = ((), (), s32[]{:S(2)}) async-start(), calls=%async_computation.30 | async-start | bytes 1179648 | tf_op jit(solution)/shard_map/reduce_scatter | solution.py:109
  393.4 280.0 %reduce-scatter.23.cloned.1.call-start = ((), (), s32[]{:S(2)}) async-start(), calls=%async_computation.31 | async-start | bytes 1179648 | tf_op jit(solution)/shard_map/reduce_scatter | solution.py:109
  405.1 3.3 copy-start.25
  408.4 4.1 copy-start.3
  412.2 8.5 %copy-start = (bf16[2048,256]{0,1:T(8,128)(2,1)S(1)}, bf16[2048,256]{0,1:T(8,128)(2,1)}, u32[]{:S(2)}) copy-start(bf16[2048,256]{0,1:T(8,128)(2,1)} %copy.306) | copy-start | bytes 3145732
  412.3 304.6 %reduce-scatter.17.cloned.1.call-start = ((), (), s32[]{:S(2)}) async-start(), calls=%async_computation.28 | async-start | bytes 1179648 | tf_op jit(solution)/shard_map/reduce_scatter | solution.py:109
  424.0 4.0 copy-start.1
  424.0 4.0 copy-start.22
  429.2 8.6 %copy-start.5 = (bf16[2048,256]{0,1:T(8,128)(2,1)S(1)}, bf16[2048,256]{0,1:T(8,128)(2,1)}, u32[]{:S(2)}) copy-start(bf16[2048,256]{0,1:T(8,128)(2,1)} %copy.280) | copy-start | bytes 3145732
  446.9 10.1 %all-to-all-start.3 = ((bf16[2,128,1,1024]{3,1,2,0:T(8,128)(2,1)}), bf16[2,128,1,1024]{3,1,2,0:T(8,128)(2,1)S(1)}, u32[]{:S(2)}, u32[]{:S(2)}) async-start(bf16[2,128,1,1024]{3,1,2,0:T(8,128)(2,1)} %maximum_bitcast_fusion), calls=%async_computation.3 | async-start | bytes 1048576 | tf_op jit(solution)/shard_map/all_to_all | solution.py:36
  456.5 15.0 %copy-start.16 = (f32[1,2048]{1,0:T(1,128)S(1)}, f32[1,2048]{1,0:T(1,128)}, u32[]{:S(2)}) copy-start(f32[1,2048]{1,0:T(1,128)} %get-tuple-element.56) | copy-start | bytes 24580
  456.5 15.0 %copy-start.17 = (f32[1,2048]{1,0:T(1,128)S(1)}, f32[1,2048]{1,0:T(1,128)}, u32[]{:S(2)}) copy-start(f32[1,2048]{1,0:T(1,128)} %get-tuple-element.57) | copy-start | bytes 24580
  456.5 15.0 %copy-start.18 = (f32[1,2048]{1,0:T(1,128)S(1)}, f32[1,2048]{1,0:T(1,128)}, u32[]{:S(2)}) copy-start(f32[1,2048]{1,0:T(1,128)} %get-tuple-element.58) | copy-start | bytes 24580
  456.5 15.0 %copy-start.19 = (f32[1,2048]{1,0:T(1,128)S(1)}, f32[1,2048]{1,0:T(1,128)}, u32[]{:S(2)}) copy-start(f32[1,2048]{1,0:T(1,128)} %get-tuple-element.59) | copy-start | bytes 24580
  456.5 15.1 %copy-start.20 = (f32[1,2048]{1,0:T(1,128)S(1)}, f32[1,2048]{1,0:T(1,128)}, u32[]{:S(2)}) copy-start(f32[1,2048]{1,0:T(1,128)} %get-tuple-element.60) | copy-start | bytes 24580
  457.0 5.7 all-to-all-start.5
  461.6 2.5 collective-permute-start
  461.6 9.9 %collective-permute-start.1 = (bf16[3,2048]{0,1:T(8,128)(2,1)S(1)}, bf16[3,2048]{0,1:T(8,128)(2,1)S(1)}, u32[]{:S(2)}, u32[]{:S(2)}) collective-permute-start(bf16[3,2048]{0,1:T(8,128)(2,1)S(1)} %bitcast.222), channel_id=1, source_target_pairs={{1,0},{2,1},{3,2},{4,3},{5,4},{6,5},{7,6},{8,7},{9,8},{10,9},{11,1... | collective-permute-start | bytes 36872 | tf_op jit(solution)/shard_map/ppermute | solution.py:23
  (3 other events, 7.7 us)
Sparse Core Ops, SparseCore 0:
  16.9 45.7 all-gather.12
  64.6 40.9 all-gather.14
  107.3 41.1 all-gather.16
  150.2 41.1 all-gather.18
  193.0 40.7 all-gather.20
  236.0 41.3 all-gather.22
  279.2 40.2 all-gather.8
  321.9 41.9 all-gather.10
  366.4 41.0 reduce-scatter.10
  409.9 41.2 reduce-scatter.12
  453.7 44.8 reduce-scatter.14
  501.0 42.0 reduce-scatter.8
  545.7 40.9 reduce-scatter.18
  589.0 40.9 reduce-scatter.20
  632.4 40.9 reduce-scatter.22
  675.8 40.9 reduce-scatter.16

commit v2 on v1

v2 whole, which is shorter than its diff:
```python
import math

import jax
import jax.numpy as jnp
import numpy as np
from jax import lax
from jax.sharding import Mesh
from jax.sharding import PartitionSpec as P

HD = 128
TAPS = 7
GROUP_HEADS = 2

SEQ = ("sc", "core")


def padded(value, width):
    peers = lax.axis_size("sc") * lax.axis_size("core")
    length = value.shape[0]
    up = [(i, (i + 1) % peers) for i in range(peers)]
    down = [(j, i) for i, j in up]
    before = lax.ppermute(value[length - width :], SEQ, up)
    after = lax.ppermute(value[:width], SEQ, down)
    return jnp.concatenate([before, value, after], axis=0)


def to_chip_rows(value):
    rows, channels = value.shape
    split = value.reshape(rows, 2, channels // 2)
    return lax.all_to_all(split, "core", 1, 0, tiled=True).reshape(2 * rows, channels // 2)


def from_chip_rows(value):
    rows2, half = value.shape
    split = value.reshape(2, rows2 // 2, 1, half)
    out = lax.all_to_all(split, "core", 0, 2, tiled=True)
    return out.reshape(rows2 // 2, 2 * half)


def butterfly_sum(value):
    axes = ("dp", "sc", "core")
    peers = 1
    for axis in axes:
        peers *= lax.axis_size(axis)
    bit = 1
    while bit < peers:
        pairs = [(i, i ^ bit) for i in range(peers)]
        value = value + lax.ppermute(value, axes, pairs)
        bit *= 2
    return value


def on_device(queries, key_states, value_states, cotangent, filter_taps):
    tok_rows = queries.shape[1]
    channels = queries.shape[2]
    chips = lax.axis_size("sc")
    seq_total = tok_rows * chips * 2
    chip_rows = 2 * tok_rows
    half_channels = channels // 2
    head_count = half_channels // HD
    group_width = GROUP_HEADS * HD
    group_count = head_count // GROUP_HEADS
    score_scale = HD ** (-0.5)
    half_width = (TAPS - 1) // 2
    local_q = queries[0]
    local_k = key_states[0]
    local_v = value_states[0]
    local_g = cotangent[0]
    grad_pad = padded(local_g, half_width)
    grad_sum = jnp.zeros((tok_rows, channels), jnp.float32)
    for tap_index in range(TAPS):
        start_row = 2 * half_width - tap_index
        grad_sum = grad_sum + filter_taps[tap_index] * grad_pad[
            start_row : start_row + tok_rows
        ].astype(jnp.float32)
    grad_attn = grad_sum.astype(jnp.bfloat16)

    stacked = jnp.stack([local_q, local_k, local_v, grad_attn], 0)
    stacked = stacked.reshape(4, tok_rows, 2, half_channels)
    stacked = lax.all_to_all(stacked, "core", 2, 1, tiled=True)
    stacked = stacked.reshape(4, chip_rows, half_channels)
    chip_q, chip_k, chip_v, chip_d = stacked[0], stacked[1], stacked[2], stacked[3]

    kv_all = lax.all_gather(
        jnp.concatenate([chip_k, chip_v], axis=1), "sc", axis=0, tiled=True
    )
    k_heads = kv_all[:, :half_channels].reshape(seq_total, head_count, HD)
    v_heads = kv_all[:, half_channels:].reshape(seq_total, head_count, HD)
    q_heads = chip_q.reshape(chip_rows, head_count, HD)
    d_heads = chip_d.reshape(chip_rows, head_count, HD)

    chip_index = lax.axis_index("sc")
    query_pos = chip_index * chip_rows + jnp.arange(chip_rows, dtype=jnp.int32)
    key_pos = jnp.arange(seq_total, dtype=jnp.int32)
    visible = query_pos[:, None] >= key_pos[None, :]

    scores = (
        jnp.einsum("thd,uhd->htu", q_heads, k_heads, preferred_element_type=jnp.float32)
        * score_scale
    )
    row_top = jnp.max(jnp.where(visible, scores, -jnp.inf), -1, keepdims=True)
    raw = jnp.where(visible, jnp.exp(scores - row_top), 0.0)
    row_total = jnp.sum(raw, -1, keepdims=True)
    probs = raw / row_total
    probs_low = probs.astype(jnp.bfloat16)
    attended = jnp.einsum("htu,uhd->thd", probs_low, v_heads, preferred_element_type=jnp.float32)
    attended = attended.astype(jnp.bfloat16).reshape(chip_rows, half_channels)
    attn_out = from_chip_rows(attended)

    out_pad = padded(attn_out, half_width)
    conv_sum = jnp.zeros((tok_rows, channels), jnp.float32)
    filter_rows = []
    local_gf = local_g.astype(jnp.float32)
    for tap_index in range(TAPS):
        moved = out_pad[tap_index : tap_index + tok_rows].astype(jnp.float32)
        conv_sum = conv_sum + filter_taps[tap_index] * moved
        filter_rows.append(jnp.sum(moved * local_gf, 0))
    filter_gradient = butterfly_sum(jnp.stack(filter_rows, 0))
    conv_output = conv_sum.astype(jnp.bfloat16)

    dprob = jnp.einsum("thd,uhd->htu", d_heads, v_heads, preferred_element_type=jnp.float32)
    row_delta = jnp.sum(probs * dprob, -1, keepdims=True)
    dscore = (probs * (dprob - row_delta) * score_scale).astype(jnp.bfloat16)
    grad_q = jnp.einsum("htu,uhd->thd", dscore, k_heads, preferred_element_type=jnp.float32)
    grad_q = grad_q.astype(jnp.bfloat16).reshape(chip_rows, half_channels)
    key_term = jnp.einsum("htu,thd->uhd", dscore, q_heads, preferred_element_type=jnp.float32)
    value_term = jnp.einsum("htu,thd->uhd", probs_low, d_heads, preferred_element_type=jnp.float32)
    kv_terms = jnp.concatenate(
        [
            key_term.astype(jnp.bfloat16).reshape(seq_total, half_channels),
            value_term.astype(jnp.bfloat16).reshape(seq_total, half_channels),
        ],
        axis=1,
    )
    kv_grads = lax.psum_scatter(kv_terms, "sc", scatter_dimension=0, tiled=True)
    back = jnp.stack(
        [grad_q, kv_grads[:, :half_channels], kv_grads[:, half_channels:]], 0
    ).reshape(3, 2, tok_rows, 1, half_channels)
    back = lax.all_to_all(back, "core", 1, 3, tiled=True).reshape(3, tok_rows, channels)
    return (
        conv_output[None],
        back[0][None],
        back[1][None],
        back[2][None],
        filter_gradient,
    )


def solution(mesh):
    devices = np.asarray(mesh.devices)
    dp_size, seq_size = devices.shape
    split_mesh = Mesh(devices.reshape(dp_size, seq_size // 2, 2), ("dp", "sc", "core"))
    block = P("dp", SEQ, None)
    in_specs = (block, block, block, block, P())
    out_specs = (block, block, block, block, P())
    return jax.shard_map(
        on_device, mesh=split_mesh, in_specs=in_specs, out_specs=out_specs, check_vma=False
    )
```

time: 750 us -> 505 us (0.67); the launches traced: 741 us -> 504 us
  waiting for transfers between devices: 404 us -> 293 us
  blocking collectives: 110 us -> 18.2 us
  matrix products: 136 us -> 91.8 us
    reduce_scatter x8 -> x1, waiting for transfers between devices: 154 us -> 53.3 us  [on_device(): kv_grads = lax.psum_scatter(kv_terms, 'sc', scatter_dimension=0, tiled=True)]
    psum x1 -> x0, blocking collectives: 81.5 us -> none  [on_device(): filter_gradient = lax.psum(jnp.stack(filter_rows, 0), ('dp', 'sc', 'core'))]
    all_gather x8 -> x1, waiting for transfers between devices: 217 us -> 171 us  [on_device(): lax.all_gather(jnp.concatenate([chip_k, chip_v], axis=1), 'sc', axis=0, t...]
    ppermute x2, waiting for transfers between devices: 1.06 us -> 36.8 us  [padded(): before = lax.ppermute(value[length - width:], SEQ, up)]
    dot_general x20 -> x5, matrix products: 111 us -> 76.7 us  [the longest x1 25.1 us: on_device(): jnp.einsum('htu,thd->uhd', dscore, q_heads, preferred_element_type=jnp.fl...]
    ppermute x0 -> x8, waiting for transfers between devices: none -> 23.4 us  [butterfly_sum(): value = value + lax.ppermute(value, axes, pairs)]
    ppermute x0 -> x8, starting transfers between devices: none -> 20.5 us  [butterfly_sum(): value = value + lax.ppermute(value, axes, pairs)]
    ppermute x2, waiting for transfers between devices: 28 us -> 8.57 us  [padded(): after = lax.ppermute(value[:width], SEQ, down)]
  transfers between devices with their start and end apart: 23 -> 14, of which waited for: 15 -> 12; matrix products, arithmetic and copies ran while one was open for 25% -> 10% of each run, Pallas kernels for 0% -> 0%
where the time goes in v2:
time: 505 us; the launch traced here: 504 us
  waiting for transfers between devices  293 us (58%)
  matrix products  91.8 us (18%)
  local copies, waits for them, and re-layouts  38.9 us (8%)
  starting transfers between devices  24.6 us (5%)
  other arithmetic  23.2 us (5%)
  blocking collectives  18.2 us (4%)
  between operations  14.3 us (3%)
    all_gather x1, waiting for transfers between devices, on_device(): lax.all_gather(jnp.concatenate([chip_k, chip_v], axis=1), 'sc', axis=0, t...  171 us
    reduce_scatter x1, waiting for transfers between devices, on_device(): kv_grads = lax.psum_scatter(kv_terms, 'sc', scatter_dimension=0, tiled=True)  53.3 us
    ppermute x2, waiting for transfers between devices, padded(): before = lax.ppermute(value[length - width:], SEQ, up)  36.8 us
    dot_general x1, matrix products, on_device(): jnp.einsum('htu,thd->uhd', dscore, q_heads, preferred_element_type=jnp.fl...  25.1 us
    dot_general x1, matrix products, on_device(): jnp.einsum('htu,uhd->thd', dscore, k_heads, preferred_element_type=jnp.fl...  24.2 us
    ppermute x8, waiting for transfers between devices, butterfly_sum(): value = value + lax.ppermute(value, axes, pairs)  23.4 us
    ppermute x8, starting transfers between devices, butterfly_sum(): value = value + lax.ppermute(value, axes, pairs)  20.5 us
    sub x1, matrix products, on_device(): raw = jnp.where(visible, jnp.exp(scores - row_top), 0.0)  15.1 us
  transfers between devices with their start and end apart: 14, of which 12 were waited for; matrix products, arithmetic and copies ran while one was open for 10% of the time, Pallas kernels for 0%

profile of v2, /device:TPU:1, one launch (start us, length us, event | category | flops | bytes accessed | tf_op | source)
XLA Modules:
  0.0 504.2 jit_solution(18042922636476511186)
XLA Ops:
  7.2 1.3 copy.65
  8.7 3.3 collective-permute-start
  12.1 1.2 fusion.82
  13.3 1.3 copy.62
  14.6 2.0 copy.63
  16.6 2.0 copy.64
  18.7 5.3 %collective-permute-done = bf16[3,2048]{0,1:T(8,128)(2,1)S(1)} collective-permute-done((bf16[3,2048]{0,1:T(8,128)(2,1)S(1)}, bf16[3,2048]{0,1:T(8,128)(2,1)S(1)}, u32[]{:S(2)}, u32[]{:S(2)}) %collective-permute-start) | collective-permute-done | bytes 12320 | tf_op jit(solution)/shard_map/ppermute | solution.py:23
  24.0 3.7 fusion.53
  27.8 1.5 pad_maximum_fusion.1
  29.2 2.7 copy.68
  32.0 6.6 %all_to_all.45 = bf16[4,128,2,1024]{3,1,0,2:T(8,128)(2,1)S(1)} all-to-all(bf16[4,128,2,1024]{3,1,0,2:T(8,128)(2,1)} %copy.68), channel_id=1, replica_groups=mesh['dp'=16,'sc'=8,'core'=2] {'core'}, dimensions={2} | all-to-all | bytes 4194304 | tf_op jit(solution)/shard_map/all_to_all | solution.py:80
  39.2 1.1 pad_maximum_fusion.3
  41.8 171.1 %all-gather.2.cloned.1.call-done = bf16[2048,2048]{0,1:T(8,128)(2,1)} async-done(((bf16[256,2048]{0,1:T(8,128)(2,1)}), bf16[2048,2048]{0,1:T(8,128)(2,1)}) %all-gather.2.cloned.1.call-update) | async-done | bytes 8388624 | tf_op jit(solution)/shard_map/all_gather | solution.py:84
  212.9 5.2 %fusion.77 = (bf16[2048,1024]{0,1:T(8,128)(2,1)}, bf16[2048,1024]{0,1:T(8,128)(2,1)S(1)}) fusion(bf16[2048,2048]{0,1:T(8,128)(2,1)} %all-gather.2.cloned.1.call-done), kind=kLoop, calls=%fused_computation.103 | loop fusion | bytes 16777216 | tf_op jit(solution)/shard_map/slice | solution.py:87
  218.1 8.1 %fusion.84 = f32[8,256,2048]{2,1,0:T(8,128)} fusion(bf16[256,8,128]{0,2,1:T(8,128)(2,1)S(1)} %copy.77, bf16[2048,8,128]{0,2,1:T(8,128)(2,1)S(1)} %bitcast.91), kind=kOutput, calls=%fused_computation.110 | convolution fusion | flops 1073741824 | bytes 21495808 | tf_op jit(solution)/shard_map/thd,uhd->htu/dot_general | solution.py:121
  226.2 15.1 %fusion.83 = (f32[8,256]{1,0:T(8,128)S(1)}, f32[8,256,2048]{2,1,0:T(8,128)}) fusion(pred[256,2048]{1,0:T(8,128)(4,1)S(1)} %iota_compare_fusion, bf16[256,8,128]{0,2,1:T(8,128)(2,1)S(1)} %copy.76, bf16[2048,8,128]{0,2,1:T(8,128)(2,1)} %bitcast.102), kind=kOutput, calls=%fused_computation.109 | convolution fusion | flops 2172651520 | bytes 22028288 | tf_op jit(solution)/shard_map/sub | solution.py:102
  241.3 9.3 %fusion.24 = bf16[8,128,2048]{2,1,0:T(8,128)(2,1)} fusion(bf16[256,8,128]{0,2,1:T(8,128)(2,1)S(1)} %copy.77, f32[8,256,2048]{2,1,0:T(8,128)} %get-tuple-element.47, f32[8,256]{1,0:T(8,128)S(1)} %get-tuple-element.46), kind=kOutput, calls=%fused_computation.22 | convolution fusion | flops 1084227584 | bytes 21504000 | tf_op jit(solution)/shard_map/htu,thd->uhd/dot_general | solution.py:127
  250.6 25.1 %fusion.27 = bf16[8,128,2048]{2,1,0:T(8,128)(2,1)} fusion(bf16[256,8,128]{0,2,1:T(8,128)(2,1)S(1)} %copy.76, f32[8,256,2048]{2,1,0:T(8,128)} %fusion.84, f32[8,256,2048]{2,1,0:T(8,128)} %get-tuple-element.47, f32[8,256]{1,0:T(8,128)S(1)} %get-tuple-element.46), kind=kOutput, calls=%fused_computation.23 | convolution fusion | flops 1105203200 | bytes 38281216 | tf_op jit(solution)/shard_map/htu,thd->uhd/dot_general | solution.py:126
  275.7 6.4 %copy.78 = bf16[2048,1024]{1,0:T(8,128)(2,1)} copy(bf16[2048,1024]{0,1:T(8,128)(2,1)} %bitcast.101) | data formatting | bytes 8388608 | tf_op jit(solution)/shard_map/reshape | solution.py:130
  282.1 6.4 %copy.79 = bf16[2048,1024]{1,0:T(8,128)(2,1)} copy(bf16[2048,1024]{0,1:T(8,128)(2,1)} %bitcast.100) | data formatting | bytes 8388608 | tf_op jit(solution)/shard_map/reshape | solution.py:131
  288.5 8.1 %pad_maximum_fusion = bf16[2048,2048]{1,0:T(8,128)(2,1)} fusion(bf16[2048,1024]{1,0:T(8,128)(2,1)} %copy.79, bf16[2048,1024]{1,0:T(8,128)(2,1)} %copy.78), kind=kLoop, calls=%fused_computation.11 | loop fusion | flops 16777216 | bytes 16777216 | tf_op jit(solution)/shard_map/concatenate | solution.py:128
  296.7 1.0 copy-done.1
  297.9 10.0 %fusion.39 = bf16[256,8,128]{0,2,1:T(8,128)(2,1)S(1)} fusion(bf16[2048,8,128]{0,2,1:T(8,128)(2,1)} %bitcast.92, f32[8,256,2048]{2,1,0:T(8,128)} %get-tuple-element.47, f32[8,256]{1,0:T(8,128)S(1)} %get-tuple-element.46), kind=kOutput, calls=%fused_computation.43 | convolution fusion | flops 1082392576 | bytes 21504000 | tf_op jit(solution)/shard_map/htu,uhd->thd/dot_general | solution.py:106
  308.2 6.3 %all_to_all.46 = bf16[2,128,1,1024]{1,3,2,0:T(8,128)(2,1)S(1)} all-to-all(bf16[2,128,1,1024]{1,3,2,0:T(8,128)(2,1)S(1)} %copy.73), channel_id=1, replica_groups=mesh['dp'=16,'sc'=8,'core'=2] {'core'}, dimensions={0} | all-to-all | bytes 1048576 | tf_op jit(solution)/shard_map/all_to_all | solution.py:36
  315.7 36.8 %collective-permute-done.2 = bf16[3,2048]{0,1:T(8,128)(2,1)S(1)} collective-permute-done((bf16[3,2048]{0,1:T(8,128)(2,1)S(1)}, bf16[3,2048]{0,1:T(8,128)(2,1)S(1)}, u32[]{:S(2)}, u32[]{:S(2)}) %collective-permute-start.2) | collective-permute-done | bytes 12320 | tf_op jit(solution)/shard_map/ppermute | solution.py:22
  352.5 3.3 collective-permute-done.3
  355.8 3.4 fusion.59
  359.4 1.2 collective-permute-done.4
  360.7 10.9 %collective-permute-done.5 = f32[7,2048]{1,0:T(8,128)S(1)} collective-permute-done((f32[7,2048]{1,0:T(8,128)S(1)}, f32[7,2048]{1,0:T(8,128)S(1)}, u32[]{:S(2)}, u32[]{:S(2)}) %collective-permute-start.5) | collective-permute-done | bytes 57376 | tf_op jit(solution)/shard_map/ppermute | solution.py:48
  371.6 4.3 collective-permute-start.6
  375.9 2.6 collective-permute-done.6
  378.5 1.1 collective-permute-start.7
  379.7 3.6 collective-permute-done.7
  383.3 1.5 collective-permute-start.8
  384.8 2.1 collective-permute-done.8
  386.9 2.5 collective-permute-start.9
  389.4 1.7 collective-permute-done.9
  391.1 6.3 %collective-permute-start.10 = (f32[7,2048]{1,0:T(8,128)S(1)}, f32[7,2048]{1,0:T(8,128)S(1)}, u32[]{:S(2)}, u32[]{:S(2)}) collective-permute-start(f32[7,2048]{1,0:T(8,128)S(1)} %add.91), channel_id=1, source_target_pairs={{0,64},{1,65},{2,66},{3,67},{4,68},{5,69},{6,70},{7,71},{8,72},{9,... | collective-permute-start | bytes 172040 | tf_op jit(solution)/shard_map/ppermute | solution.py:48
  397.4 24.2 %fusion.36 = bf16[256,8,128]{0,2,1:T(8,128)(2,1)S(1)} fusion(bf16[2048,8,128]{0,2,1:T(8,128)(2,1)} %bitcast.103, f32[8,256,2048]{2,1,0:T(8,128)} %fusion.84, f32[8,256,2048]{2,1,0:T(8,128)} %get-tuple-element.47, f32[8,256]{1,0:T(8,128)S(1)} %get-tuple-element.46), kind=kOutput, calls=%fused_computation.42 | convolution fusion | flops 1103368192 | bytes 38281216 | tf_op jit(solution)/shard_map/htu,uhd->thd/dot_general | solution.py:124
  422.2 4.4 collective-permute-start.11
  426.6 3.7 fusion.68
  430.3 1.0 copy.85
  431.3 1.4 collective-permute-done.11
  433.3 53.3 %reduce-scatter.2.cloned.1.call-done = bf16[256,2048]{1,0:T(8,128)(2,1)} async-done(((bf16[2048,2048]{1,0:T(8,128)(2,1)}), bf16[256,2048]{1,0:T(8,128)(2,1)}) %reduce-scatter.2.cloned.1.call-update) | async-done | bytes 1048592 | tf_op jit(solution)/shard_map/reduce_scatter | solution.py:135
  486.6 1.3 fusion.80
  489.0 5.2 %all_to_all.47 = bf16[3,2,128,1,1024]{2,4,3,0,1:T(8,128)(2,1)S(1)} all-to-all(bf16[3,2,128,1,1024]{2,4,3,0,1:T(8,128)(2,1)S(1)} %copy.81), channel_id=1, replica_groups=mesh['dp'=16,'sc'=8,'core'=2] {'core'}, dimensions={1} | all-to-all | bytes 3145728 | tf_op jit(solution)/shard_map/all_to_all | solution.py:139
  494.3 1.0 copy.86
  495.3 1.0 copy.87
  (45 shorter events, 7.6 us)
Async XLA Ops:
  7.2 205.8 %all-gather.2.cloned.1.call-start = ((), (), s32[]{:S(2)}) async-start(), calls=%async_computation.4 | async-start | bytes 9437184 | tf_op jit(solution)/shard_map/all_gather | solution.py:84
  8.7 15.2 %collective-permute-start = (bf16[3,2048]{0,1:T(8,128)(2,1)S(1)}, bf16[3,2048]{0,1:T(8,128)(2,1)S(1)}, u32[]{:S(2)}, u32[]{:S(2)}) collective-permute-start(bf16[3,2048]{0,1:T(8,128)(2,1)S(1)} %get-tuple-element.37), channel_id=1, source_target_pairs={{1,0},{2,1},{3,2},{4,3},{5,4},{6,5},{7,6},{8,7},{9,8},{10,9},{11,1... | collective-permute-start | bytes 36872 | tf_op jit(solution)/shard_map/ppermute | solution.py:23
  12.1 11.9 %collective-permute-start.1 = (bf16[3,2048]{0,1:T(8,128)(2,1)S(1)}, bf16[3,2048]{0,1:T(8,128)(2,1)S(1)}, u32[]{:S(2)}, u32[]{:S(2)}) collective-permute-start(bf16[3,2048]{0,1:T(8,128)(2,1)S(1)} %get-tuple-element.38), channel_id=1, source_target_pairs={{0,1},{1,2},{2,3},{3,4},{4,5},{5,6},{6,7},{7,8},{8,9},{9,10},{10,1... | collective-permute-start | bytes 36872 | tf_op jit(solution)/shard_map/ppermute | solution.py:22
  40.3 446.3 %reduce-scatter.2.cloned.1.call-start = ((), (), s32[]{:S(2)}) async-start(), calls=%async_computation.5 | async-start | bytes 9437184 | tf_op jit(solution)/shard_map/reduce_scatter | solution.py:135
  218.1 8.1 %copy-start = (bf16[2048,1024]{0,1:T(8,128)(2,1)}, bf16[2048,1024]{0,1:T(8,128)(2,1)S(1)}, u32[]{:S(2)}) copy-start(bf16[2048,1024]{0,1:T(8,128)(2,1)S(1)} %get-tuple-element.25) | copy-start | bytes 12582916
  296.7 1.0 copy-start.1
  314.7 37.8 %collective-permute-start.2 = (bf16[3,2048]{0,1:T(8,128)(2,1)S(1)}, bf16[3,2048]{0,1:T(8,128)(2,1)S(1)}, u32[]{:S(2)}, u32[]{:S(2)}) collective-permute-start(bf16[3,2048]{0,1:T(8,128)(2,1)S(1)} %bitcast.120), channel_id=1, source_target_pairs={{0,1},{1,2},{2,3},{3,4},{4,5},{5,6},{6,7},{7,8},{8,9},{9,10},{10,1... | collective-permute-start | bytes 36872 | tf_op jit(solution)/shard_map/ppermute | solution.py:22
  314.8 40.9 %collective-permute-start.3 = (bf16[3,2048]{0,1:T(8,128)(2,1)S(1)}, bf16[3,2048]{0,1:T(8,128)(2,1)S(1)}, u32[]{:S(2)}, u32[]{:S(2)}) collective-permute-start(bf16[3,2048]{0,1:T(8,128)(2,1)S(1)} %bitcast.119), channel_id=1, source_target_pairs={{1,0},{2,1},{3,2},{4,3},{5,4},{6,5},{7,6},{8,7},{9,8},{10,9},{11,1... | collective-permute-start | bytes 36872 | tf_op jit(solution)/shard_map/ppermute | solution.py:23
  359.3 1.3 collective-permute-start.4
  360.6 11.0 %collective-permute-start.5 = (f32[7,2048]{1,0:T(8,128)S(1)}, f32[7,2048]{1,0:T(8,128)S(1)}, u32[]{:S(2)}, u32[]{:S(2)}) collective-permute-start(f32[7,2048]{1,0:T(8,128)S(1)} %add.86), channel_id=1, source_target_pairs={{0,2},{1,3},{2,0},{3,1},{4,6},{5,7},{6,4},{7,5},{8,10},{9,11},{10,... | collective-permute-start | bytes 172040 | tf_op jit(solution)/shard_map/ppermute | solution.py:48
  371.6 6.9 %collective-permute-start.6 = (f32[7,2048]{1,0:T(8,128)S(1)}, f32[7,2048]{1,0:T(8,128)S(1)}, u32[]{:S(2)}, u32[]{:S(2)}) collective-permute-start(f32[7,2048]{1,0:T(8,128)S(1)} %add.87), channel_id=1, source_target_pairs={{0,4},{1,5},{2,6},{3,7},{4,0},{5,1},{6,2},{7,3},{8,12},{9,13},{10,... | collective-permute-start | bytes 172040 | tf_op jit(solution)/shard_map/ppermute | solution.py:48
  378.5 4.7 collective-permute-start.7
  383.3 3.6 collective-permute-start.8
  386.9 4.2 collective-permute-start.9
  391.1 31.1 %collective-permute-start.10 = (f32[7,2048]{1,0:T(8,128)S(1)}, f32[7,2048]{1,0:T(8,128)S(1)}, u32[]{:S(2)}, u32[]{:S(2)}) collective-permute-start(f32[7,2048]{1,0:T(8,128)S(1)} %add.91), channel_id=1, source_target_pairs={{0,64},{1,65},{2,66},{3,67},{4,68},{5,69},{6,70},{7,71},{8,72},{9,... | collective-permute-start | bytes 172040 | tf_op jit(solution)/shard_map/ppermute | solution.py:48
  422.2 10.5 %collective-permute-start.11 = (f32[7,2048]{1,0:T(8,128)S(1)}, f32[7,2048]{1,0:T(8,128)S(1)}, u32[]{:S(2)}, u32[]{:S(2)}) collective-permute-start(f32[7,2048]{1,0:T(8,128)S(1)} %add.92), channel_id=1, source_target_pairs={{0,128},{1,129},{2,130},{3,131},{4,132},{5,133},{6,134},{7,135},{8... | collective-permute-start | bytes 172040 | tf_op jit(solution)/shard_map/ppermute | solution.py:48
Sparse Core Ops, SparseCore 0:
  40.4 172.4 all-gather.1
  296.8 189.7 reduce-scatter.1

commit v3 on v2

v3 whole, which is shorter than its diff:
```python
import jax
import jax.numpy as jnp
from jax import lax
from jax.sharding import PartitionSpec as P

HD = 128
TAPS = 7


def padded(value, width):
    peers = lax.axis_size("seq")
    length = value.shape[0]
    up = [(i, (i + 1) % peers) for i in range(peers)]
    down = [(j, i) for i, j in up]
    before = lax.ppermute(value[length - width :], "seq", up)
    after = lax.ppermute(value[:width], "seq", down)
    return jnp.concatenate([before, value, after], axis=0)


def butterfly_sum(value):
    axes = ("dp", "seq")
    peers = lax.axis_size("dp") * lax.axis_size("seq")
    bit = 1
    while bit < peers:
        pairs = [(i, i ^ bit) for i in range(peers)]
        value = value + lax.ppermute(value, axes, pairs)
        bit *= 2
    return value


def on_device(queries, key_states, value_states, cotangent, filter_taps):
    tok_rows = queries.shape[1]
    channels = queries.shape[2]
    seq_total = tok_rows * lax.axis_size("seq")
    head_count = channels // HD
    score_scale = HD ** (-0.5)
    half_width = (TAPS - 1) // 2
    local_q = queries[0]
    local_k = key_states[0]
    local_v = value_states[0]
    local_g = cotangent[0]
    grad_pad = padded(local_g, half_width)
    grad_sum = jnp.zeros((tok_rows, channels), jnp.float32)
    for tap_index in range(TAPS):
        start_row = 2 * half_width - tap_index
        grad_sum = grad_sum + filter_taps[tap_index] * grad_pad[
            start_row : start_row + tok_rows
        ].astype(jnp.float32)
    grad_attn = grad_sum.astype(jnp.bfloat16)

    key_all = lax.all_gather(local_k, "seq", axis=0, tiled=True)
    value_all = lax.all_gather(local_v, "seq", axis=0, tiled=True)
    q_heads = local_q.reshape(tok_rows, head_count, HD)
    d_heads = grad_attn.reshape(tok_rows, head_count, HD)
    k_heads = key_all.reshape(seq_total, head_count, HD)
    v_heads = value_all.reshape(seq_total, head_count, HD)

    device_index = lax.axis_index("seq")
    query_pos = device_index * tok_rows + jnp.arange(tok_rows, dtype=jnp.int32)
    key_pos = jnp.arange(seq_total, dtype=jnp.int32)
    visible = query_pos[:, None] >= key_pos[None, :]

    scores = (
        jnp.einsum("thd,uhd->htu", q_heads, k_heads, preferred_element_type=jnp.float32)
        * score_scale
    )
    row_top = jnp.max(jnp.where(visible, scores, -jnp.inf), -1, keepdims=True)
    raw = jnp.where(visible, jnp.exp(scores - row_top), 0.0)
    row_total = jnp.sum(raw, -1, keepdims=True)
    probs = raw / row_total
    probs_low = probs.astype(jnp.bfloat16)
    attended = jnp.einsum("htu,uhd->thd", probs_low, v_heads, preferred_element_type=jnp.float32)
    attn_out = attended.astype(jnp.bfloat16).reshape(tok_rows, channels)

    out_pad = padded(attn_out, half_width)
    conv_sum = jnp.zeros((tok_rows, channels), jnp.float32)
    filter_rows = []
    local_gf = local_g.astype(jnp.float32)
    for tap_index in range(TAPS):
        moved = out_pad[tap_index : tap_index + tok_rows].astype(jnp.float32)
        conv_sum = conv_sum + filter_taps[tap_index] * moved
        filter_rows.append(jnp.sum(moved * local_gf, 0))
    filter_gradient = butterfly_sum(jnp.stack(filter_rows, 0))
    conv_output = conv_sum.astype(jnp.bfloat16)

    value_term = jnp.einsum("htu,thd->uhd", probs_low, d_heads, preferred_element_type=jnp.float32)
    grad_values = lax.psum_scatter(
        value_term.astype(jnp.bfloat16).reshape(seq_total, channels),
        "seq", scatter_dimension=0, tiled=True,
    )
    dprob = jnp.einsum("thd,uhd->htu", d_heads, v_heads, preferred_element_type=jnp.float32)
    row_delta = jnp.sum(probs * dprob, -1, keepdims=True)
    dscore = (probs * (dprob - row_delta) * score_scale).astype(jnp.bfloat16)
    key_term = jnp.einsum("htu,thd->uhd", dscore, q_heads, preferred_element_type=jnp.float32)
    grad_keys = lax.psum_scatter(
        key_term.astype(jnp.bfloat16).reshape(seq_total, channels),
        "seq", scatter_dimension=0, tiled=True,
    )
    grad_q = jnp.einsum("htu,uhd->thd", dscore, k_heads, preferred_element_type=jnp.float32)
    grad_queries = grad_q.astype(jnp.bfloat16).reshape(tok_rows, channels)
    return (
        conv_output[None],
        grad_queries[None],
        grad_keys[None],
        grad_values[None],
        filter_gradient,
    )


def solution(mesh):
    block = P("dp", "seq", None)
    in_specs = (block, block, block, block, P())
    out_specs = (block, block, block, block, P())
    return jax.shard_map(
        on_device, mesh=mesh, in_specs=in_specs, out_specs=out_specs, check_vma=False
    )
```

time: 505 us -> 427 us (0.85)
  waiting for transfers between devices: 293 us -> 240 us
  matrix products: 91.8 us -> 112 us
  blocking collectives: 18.2 us -> 0 us
  starting transfers between devices: 24.6 us -> 12.8 us
  other arithmetic: 23.2 us -> 11.8 us
    all_gather x1 -> x2, waiting for transfers between devices: 171 us -> 101 us  [the longest x1 58.1 us: on_device(): key_all = lax.all_gather(local_k, 'seq', axis=0, tiled=True)]
    reduce_scatter x1 -> x2, waiting for transfers between devices: 53.3 us -> 84.7 us  [the longest x1 84.7 us: on_device(): lax.psum_scatter(value_term.astype(jnp.bfloat16).reshape(seq_total, chann...]
    all_to_all x3 -> x0, blocking collectives: 18.2 us -> none  [the longest x1 6.6 us: on_device(): stacked = lax.all_to_all(stacked, 'core', 2, 1, tiled=True)]
    ppermute x4, waiting for transfers between devices: 45.4 us -> 30.7 us  [the longest x2 27.8 us: padded(): after = lax.ppermute(value[:width], 'seq', down)]
    ppermute x8, starting transfers between devices: 20.5 us -> 7.99 us  [butterfly_sum(): value = value + lax.ppermute(value, axes, pairs)]
    reshape x2, local copies, waits for them, and re-layouts: 12.8 us -> 24.6 us  [the longest x1 12.3 us: on_device(): value_term.astype(jnp.bfloat16).reshape(seq_total, channels)]
    concatenate x2 -> x0, other arithmetic: 9.26 us -> none  [the longest x1 8.12 us: on_device(): jnp.concatenate([key_term.astype(jnp.bfloat16).reshape(seq_total, half_ch...]
    slice x6 -> x3, local copies, waits for them, and re-layouts: 7.15 us -> 0.54 us  [padded(): after = lax.ppermute(value[:width], 'seq', down)]
  transfers between devices with their start and end apart: 14 -> 16, of which waited for: 12 -> 13; matrix products, arithmetic and copies ran while one was open for 10% -> 23% of each run, Pallas kernels for 0% -> 0%
where the time goes in v3:
time: 427 us; the launch traced here: 426 us
  waiting for transfers between devices  240 us (56%)
  matrix products  112 us (26%)
  local copies, waits for them, and re-layouts  36 us (8%)
  between operations  13.9 us (3%)
  starting transfers between devices  12.8 us (3%)
  other arithmetic  11.8 us (3%)
    reduce_scatter x1, waiting for transfers between devices, on_device(): lax.psum_scatter(value_term.astype(jnp.bfloat16).reshape(seq_total, chann...  84.7 us
    all_gather x1, waiting for transfers between devices, on_device(): key_all = lax.all_gather(local_k, 'seq', axis=0, tiled=True)  58.1 us
    all_gather x1, waiting for transfers between devices, on_device(): value_all = lax.all_gather(local_v, 'seq', axis=0, tiled=True)  42.9 us
    dot_general x1, matrix products, on_device(): jnp.einsum('htu,thd->uhd', dscore, q_heads, preferred_element_type=jnp.fl...  30.3 us
    dot_general x1, matrix products, on_device(): jnp.einsum('htu,uhd->thd', dscore, k_heads, preferred_element_type=jnp.fl...  28.7 us
    ppermute x2, waiting for transfers between devices, padded(): after = lax.ppermute(value[:width], 'seq', down)  27.8 us
    ppermute x8, waiting for transfers between devices, butterfly_sum(): value = value + lax.ppermute(value, axes, pairs)  23.6 us
    sub x1, matrix products, on_device(): raw = jnp.where(visible, jnp.exp(scores - row_top), 0.0)  17.9 us
  transfers between devices with their start and end apart: 16, of which 13 were waited for; matrix products, arithmetic and copies ran while one was open for 23% of the time, Pallas kernels for 0%

profile of v3, /device:TPU:1, one launch (start us, length us, event | category | flops | bytes accessed | tf_op | source)
XLA Modules:
  0.0 426.4 jit_solution(1900943750984612184)
XLA Ops:
  7.2 2.0 copy.39
  9.3 2.0 copy.36
  11.4 1.3 copy.44
  12.8 0.2 slice_bitcast_fusion.1
  13.0 3.3 collective-permute-start.2
  16.3 0.2 iota_compare_fusion
  16.5 1.2 fusion.68
  17.8 1.3 copy.60
  19.1 10.1 %collective-permute-done.2 = bf16[3,2048]{0,1:T(8,128)(2,1)S(1)} collective-permute-done((bf16[3,2048]{0,1:T(8,128)(2,1)S(1)}, bf16[3,2048]{0,1:T(8,128)(2,1)S(1)}, u32[]{:S(2)}, u32[]{:S(2)}) %collective-permute-start.2) | collective-permute-done | bytes 12320 | tf_op jit(solution)/shard_map/ppermute | solution.py:16
  29.1 2.8 collective-permute-done.3
  31.9 3.7 fusion.46
  35.6 42.9 %all-gather.7.cloned.1.call-done = bf16[1,2048,2048]{1,2,0:T(8,128)(2,1)} async-done(((bf16[1,128,2048]{1,2,0:T(8,128)(2,1)}), bf16[1,2048,2048]{1,2,0:T(8,128)(2,1)}) %all-gather.7.cloned.1.call-update) | async-done | bytes 8388624 | tf_op jit(solution)/shard_map/all_gather | solution.py:52
  78.6 11.5 %fusion.70 = f32[16,128,2048]{2,1,0:T(8,128)} fusion(bf16[128,16,128]{0,2,1:T(8,128)(2,1)S(1)} %bitcast.69, bf16[2048,16,128]{0,2,1:T(8,128)(2,1)} %bitcast.63), kind=kOutput, calls=%fused_computation.99 | convolution fusion | flops 1073741824 | bytes 25690112 | tf_op jit(solution)/shard_map/thd,uhd->htu/dot_general | solution.py:91
  90.1 58.1 %all-gather.5.cloned.1.call-done = bf16[1,2048,2048]{1,2,0:T(8,128)(2,1)} async-done(((bf16[1,128,2048]{1,2,0:T(8,128)(2,1)}), bf16[1,2048,2048]{1,2,0:T(8,128)(2,1)}) %all-gather.5.cloned.1.call-update) | async-done | bytes 8388624 | tf_op jit(solution)/shard_map/all_gather | solution.py:51
  148.2 17.9 %fusion.69 = (f32[16,128]{1,0:T(8,128)S(1)}, f32[16,128,2048]{2,1,0:T(8,128)}) fusion(pred[128,2048]{1,0:T(8,128)(4,1)S(1)} %iota_compare_fusion, bf16[128,16,128]{0,2,1:T(8,128)(2,1)S(1)} %bitcast.71, bf16[2048,16,128]{0,2,1:T(8,128)(2,1)} %bitcast.95), kind=kOutput, calls=%fused_computation.98 | convolution fusion | flops 2172651520 | bytes 25960448 | tf_op jit(solution)/shard_map/sub | solution.py:68
  166.1 30.3 %fusion.18 = bf16[16,2048,128]{1,2,0:T(8,128)(2,1)} fusion(bf16[128,16,128]{0,2,1:T(8,128)(2,1)S(1)} %bitcast.72, f32[16,128,2048]{2,1,0:T(8,128)} %fusion.70, f32[16,128,2048]{2,1,0:T(8,128)} %get-tuple-element.41, f32[16,128]{1,0:T(8,128)S(1)} %get-tuple-element.40), kind=kOutput, calls=%fused_computation.15 | convolution fusion | flops 1107300352 | bytes 42475520 | tf_op jit(solution)/shard_map/htu,thd->uhd/dot_general | solution.py:94
  196.4 12.3 %copy.50 = bf16[2048,2048]{1,0:T(8,128)(2,1)} copy(bf16[2048,2048]{0,1:T(8,128)(2,1)} %bitcast.65) | data formatting | bytes 16777216 | tf_op jit(solution)/shard_map/reshape | solution.py:96
  208.7 0.3 reduce-scatter.5.cloned.1.call-start
  209.0 11.4 %convolution_convert_fusion = bf16[16,128,2048]{2,1,0:T(8,128)(2,1)} fusion(bf16[128,16,128]{0,2,1:T(8,128)(2,1)S(1)} %bitcast.70, f32[16,128,2048]{2,1,0:T(8,128)} %get-tuple-element.41, f32[16,128]{1,0:T(8,128)S(1)} %get-tuple-element.40), kind=kOutput, calls=%fused_computation.16 | convolution fusion | flops 1086324736 | bytes 25698304 | tf_op jit(solution)/shard_map/htu,thd->uhd/dot_general | solution.py:86
  220.3 12.3 %copy.51 = bf16[2048,2048]{1,0:T(8,128)(2,1)} copy(bf16[2048,2048]{0,1:T(8,128)(2,1)} %bitcast.66) | data formatting | bytes 16777216 | tf_op jit(solution)/shard_map/reshape | solution.py:88
  232.7 0.2 copy.53
  232.9 12.1 %multiply_reduce_fusion.1 = (f32[16,128]{1,0:T(8,128)S(1)}, bf16[128,16,128]{2,0,1:T(8,128)(2,1)S(1)}) fusion(f32[128,16,128]{2,0,1:T(8,128)S(1)} %copy.53, bf16[2048,16,128]{0,2,1:T(8,128)(2,1)} %bitcast.64, f32[16,128,2048]{2,1,0:T(8,128)} %get-tuple-element.41, f32[16,128]{1,0:T(8,128)S(1)} %get-tuple-element.40), kind=kOutput, calls=%fused_computation.71 | convolution fusion | flops 1083176960 | bytes 26755072 | tf_op jit(solution)/shard_map/htu,uhd->thd/dot_general | solution.py:72
  245.0 1.0 collective-permute-start
  246.0 0.3 copy.43
  246.4 0.3 copy.41
  246.7 0.2 collective-permute-done
  246.9 0.3 copy.42
  247.2 17.7 %collective-permute-done.1 = bf16[3,2048]{0,1:T(8,128)(2,1)S(1)} collective-permute-done((bf16[3,2048]{0,1:T(8,128)(2,1)S(1)}, bf16[3,2048]{0,1:T(8,128)(2,1)S(1)}, u32[]{:S(2)}, u32[]{:S(2)}) %collective-permute-start.1) | collective-permute-done | bytes 12320 | tf_op jit(solution)/shard_map/ppermute | solution.py:16
  264.9 3.4 fusion.52
  268.3 0.1 stack.31
  268.4 0.1 collective-permute-start.4
  268.5 1.2 collective-permute-done.4
  269.9 6.4 %collective-permute-done.5 = f32[7,2048]{1,0:T(8,128)S(1)} collective-permute-done((f32[7,2048]{1,0:T(8,128)S(1)}, f32[7,2048]{1,0:T(8,128)S(1)}, u32[]{:S(2)}, u32[]{:S(2)}) %collective-permute-start.5) | collective-permute-done | bytes 57376 | tf_op jit(solution)/shard_map/ppermute | solution.py:26
  276.3 0.4 collective-permute-start.6
  276.7 3.2 collective-permute-done.6
  280.0 5.0 %collective-permute-done.7 = f32[7,2048]{1,0:T(8,128)S(1)} collective-permute-done((f32[7,2048]{1,0:T(8,128)S(1)}, f32[7,2048]{1,0:T(8,128)S(1)}, u32[]{:S(2)}, u32[]{:S(2)}) %collective-permute-start.7) | collective-permute-done | bytes 57376 | tf_op jit(solution)/shard_map/ppermute | solution.py:26
  285.0 0.1 collective-permute-start.8
  285.2 3.5 collective-permute-done.8
  288.7 0.4 collective-permute-start.9
  289.0 4.2 collective-permute-done.9
  293.3 2.7 collective-permute-start.10
  296.0 28.7 %fusion.29 = bf16[16,128,128]{1,2,0:T(8,128)(2,1)S(1)} fusion(bf16[2048,16,128]{0,2,1:T(8,128)(2,1)} %bitcast.96, f32[16,128,2048]{2,1,0:T(8,128)} %fusion.70, f32[16,128,2048]{2,1,0:T(8,128)} %get-tuple-element.41, f32[16,128]{1,0:T(8,128)S(1)} %get-tuple-element.40), kind=kOutput, calls=%fused_computation.35 | convolution fusion | flops 1103368192 | bytes 42475520 | tf_op jit(solution)/shard_map/htu,uhd->thd/dot_general | solution.py:99
  324.7 1.0 copy.55
  325.7 4.1 collective-permute-start.11
  329.8 3.7 fusion.61
  333.6 1.0 copy.54
  334.6 0.6 add.95
  335.2 84.7 %reduce-scatter.5.cloned.1.call-done = bf16[128,2048]{1,0:T(8,128)(2,1)} async-done(((bf16[2048,2048]{1,0:T(8,128)(2,1)}), bf16[128,2048]{1,0:T(8,128)(2,1)}) %reduce-scatter.5.cloned.1.call-update) | async-done | bytes 524304 | tf_op jit(solution)/shard_map/reduce_scatter | solution.py:87
  (23 shorter events, 0.5 us)
Async XLA Ops:
  7.2 71.4 %all-gather.7.cloned.1.call-start = ((), (), s32[]{:S(2)}) async-start(), calls=%async_computation.5 | async-start | bytes 8912896 | tf_op jit(solution)/shard_map/all_gather | solution.py:52
  9.3 138.9 %all-gather.5.cloned.1.call-start = ((), (), s32[]{:S(2)}) async-start(), calls=%async_computation.4 | async-start | bytes 8912896 | tf_op jit(solution)/shard_map/all_gather | solution.py:51
  11.4 323.8 %reduce-scatter.3.cloned.1.call-start = ((), (), s32[]{:S(2)}) async-start(), calls=%async_computation.2 | async-start | bytes 8912896 | tf_op jit(solution)/shard_map/reduce_scatter | solution.py:95
  13.0 16.2 %collective-permute-start.2 = (bf16[3,2048]{0,1:T(8,128)(2,1)S(1)}, bf16[3,2048]{0,1:T(8,128)(2,1)S(1)}, u32[]{:S(2)}, u32[]{:S(2)}) collective-permute-start(bf16[3,2048]{0,1:T(8,128)(2,1)S(1)} %get-tuple-element.29), channel_id=1, source_target_pairs={{1,0},{2,1},{3,2},{4,3},{5,4},{6,5},{7,6},{8,7},{9,8},{10,9},{11,1... | collective-permute-start | bytes 36872 | tf_op jit(solution)/shard_map/ppermute | solution.py:16
  16.3 15.6 %collective-permute-start.3 = (bf16[3,2048]{0,1:T(8,128)(2,1)S(1)}, bf16[3,2048]{0,1:T(8,128)(2,1)S(1)}, u32[]{:S(2)}, u32[]{:S(2)}) collective-permute-start(bf16[3,2048]{0,1:T(8,128)(2,1)S(1)} %get-tuple-element.30), channel_id=1, source_target_pairs={{0,1},{1,2},{2,3},{3,4},{4,5},{5,6},{6,7},{7,8},{8,9},{9,10},{10,1... | collective-permute-start | bytes 36872 | tf_op jit(solution)/shard_map/ppermute | solution.py:15
  208.7 211.2 %reduce-scatter.5.cloned.1.call-start = ((), (), s32[]{:S(2)}) async-start(), calls=%async_computation.3 | async-start | bytes 8912896 | tf_op jit(solution)/shard_map/reduce_scatter | solution.py:87
  245.0 1.9 collective-permute-start
  246.3 18.6 %collective-permute-start.1 = (bf16[3,2048]{0,1:T(8,128)(2,1)S(1)}, bf16[3,2048]{0,1:T(8,128)(2,1)S(1)}, u32[]{:S(2)}, u32[]{:S(2)}) collective-permute-start(bf16[3,2048]{0,1:T(8,128)(2,1)S(1)} %copy.43), channel_id=1, source_target_pairs={{1,0},{2,1},{3,2},{4,3},{5,4},{6,5},{7,6},{8,7},{9,8},{10,9},{11,1... | collective-permute-start | bytes 36872 | tf_op jit(solution)/shard_map/ppermute | solution.py:16
  268.4 1.3 collective-permute-start.4
  269.8 6.5 %collective-permute-start.5 = (f32[7,2048]{1,0:T(8,128)S(1)}, f32[7,2048]{1,0:T(8,128)S(1)}, u32[]{:S(2)}, u32[]{:S(2)}) collective-permute-start(f32[7,2048]{1,0:T(8,128)S(1)} %add.88), channel_id=1, source_target_pairs={{0,2},{1,3},{2,0},{3,1},{4,6},{5,7},{6,4},{7,5},{8,10},{9,11},{10,... | collective-permute-start | bytes 172040 | tf_op jit(solution)/shard_map/ppermute | solution.py:26
  276.3 3.6 collective-permute-start.6
  279.9 5.1 %collective-permute-start.7 = (f32[7,2048]{1,0:T(8,128)S(1)}, f32[7,2048]{1,0:T(8,128)S(1)}, u32[]{:S(2)}, u32[]{:S(2)}) collective-permute-start(f32[7,2048]{1,0:T(8,128)S(1)} %add.90), channel_id=1, source_target_pairs={{0,8},{1,9},{2,10},{3,11},{4,12},{5,13},{6,14},{7,15},{8,0},{9,1},... | collective-permute-start | bytes 172040 | tf_op jit(solution)/shard_map/ppermute | solution.py:26
  285.0 3.6 collective-permute-start.8
  288.7 4.6 %collective-permute-start.9 = (f32[7,2048]{1,0:T(8,128)S(1)}, f32[7,2048]{1,0:T(8,128)S(1)}, u32[]{:S(2)}, u32[]{:S(2)}) collective-permute-start(f32[7,2048]{1,0:T(8,128)S(1)} %add.92), channel_id=1, source_target_pairs={{0,32},{1,33},{2,34},{3,35},{4,36},{5,37},{6,38},{7,39},{8,40},{9,... | collective-permute-start | bytes 172040 | tf_op jit(solution)/shard_map/ppermute | solution.py:26
  293.3 32.4 %collective-permute-start.10 = (f32[7,2048]{1,0:T(8,128)S(1)}, f32[7,2048]{1,0:T(8,128)S(1)}, u32[]{:S(2)}, u32[]{:S(2)}) collective-permute-start(f32[7,2048]{1,0:T(8,128)S(1)} %add.93), channel_id=1, source_target_pairs={{0,64},{1,65},{2,66},{3,67},{4,68},{5,69},{6,70},{7,71},{8,72},{9,... | collective-permute-start | bytes 172040 | tf_op jit(solution)/shard_map/ppermute | solution.py:26
  325.7 8.9 %collective-permute-start.11 = (f32[7,2048]{1,0:T(8,128)S(1)}, f32[7,2048]{1,0:T(8,128)S(1)}, u32[]{:S(2)}, u32[]{:S(2)}) collective-permute-start(f32[7,2048]{1,0:T(8,128)S(1)} %add.94), channel_id=1, source_target_pairs={{0,128},{1,129},{2,130},{3,131},{4,132},{5,133},{6,134},{7,135},{8... | collective-permute-start | bytes 172040 | tf_op jit(solution)/shard_map/ppermute | solution.py:26
Sparse Core Ops, SparseCore 0:
  10.3 68.2 all-gather.6
  80.9 67.2 all-gather.4
  208.8 105.8 reduce-scatter.2
  317.6 102.1 reduce-scatter.4

commit v4 on v3

--- a/solution.py
+++ b/solution.py
@@ -49,6 +49,7 @@
     grad_attn = grad_sum.astype(jnp.bfloat16)
 
     key_all = lax.all_gather(local_k, "seq", axis=0, tiled=True)
+    key_all, local_v = lax.optimization_barrier((key_all, local_v))
     value_all = lax.all_gather(local_v, "seq", axis=0, tiled=True)
     q_heads = local_q.reshape(tok_rows, head_count, HD)
     d_heads = grad_attn.reshape(tok_rows, head_count, HD)
@@ -69,6 +70,11 @@
     row_total = jnp.sum(raw, -1, keepdims=True)
     probs = raw / row_total
     probs_low = probs.astype(jnp.bfloat16)
+    value_term = jnp.einsum("htu,thd->uhd", probs_low, d_heads, preferred_element_type=jnp.float32)
+    grad_values = lax.psum_scatter(
+        value_term.astype(jnp.bfloat16).reshape(seq_total, channels),
+        "seq", scatter_dimension=0, tiled=True,
+    )
     attended = jnp.einsum("htu,uhd->thd", probs_low, v_heads, preferred_element_type=jnp.float32)
     attn_out = attended.astype(jnp.bfloat16).reshape(tok_rows, channels)
 
@@ -83,11 +89,6 @@
     filter_gradient = butterfly_sum(jnp.stack(filter_rows, 0))
     conv_output = conv_sum.astype(jnp.bfloat16)
 
-    value_term = jnp.einsum("htu,thd->uhd", probs_low, d_heads, preferred_element_type=jnp.float32)
-    grad_values = lax.psum_scatter(
-        value_term.astype(jnp.bfloat16).reshape(seq_total, channels),
-        "seq", scatter_dimension=0, tiled=True,
-    )
     dprob = jnp.einsum("thd,uhd->htu", d_heads, v_heads, preferred_element_type=jnp.float32)
     row_delta = jnp.sum(probs * dprob, -1, keepdims=True)
     dscore = (probs * (dprob - row_delta) * score_scale).astype(jnp.bfloat16)

time: 427 us -> 363 us (0.85)
  waiting for transfers between devices: 240 us -> 154 us
  starting transfers between devices: 12.8 us -> 27.7 us
  local copies, waits for them, and re-layouts: 36 us -> 46.3 us
    reduce_scatter x1, waiting for transfers between devices: 84.7 us -> 0.01 us  [on_device(): lax.psum_scatter(value_term.astype(jnp.bfloat16).reshape(seq_total, chann...]
    reduce_scatter x1, waiting for transfers between devices: 0.01 us -> 57.9 us  [on_device(): lax.psum_scatter(key_term.astype(jnp.bfloat16).reshape(seq_total, channel...]
    all_gather x1, waiting for transfers between devices: 42.9 us -> 0.02 us  [on_device(): value_all = lax.all_gather(local_v, 'seq', axis=0, tiled=True)]
    ppermute x8, starting transfers between devices: 7.99 us -> 23.2 us  [butterfly_sum(): value = value + lax.ppermute(value, axes, pairs)]
    ppermute x2, waiting for transfers between devices: 27.8 us -> 12.9 us  [padded(): after = lax.ppermute(value[:width], 'seq', down)]
    reshape x0 -> x1, local copies, waits for them, and re-layouts: none -> 12.3 us  [on_device(): k_heads = key_all.reshape(seq_total, head_count, HD)]
    ppermute x8, waiting for transfers between devices: 23.6 us -> 15.1 us  [butterfly_sum(): value = value + lax.ppermute(value, axes, pairs)]
    ppermute x2, waiting for transfers between devices: 2.93 us -> 8.55 us  [padded(): before = lax.ppermute(value[length - width:], 'seq', up)]
  transfers between devices with their start and end apart: 16 -> 16, of which waited for: 13 -> 11; matrix products, arithmetic and copies ran while one was open for 23% -> 46% of each run, Pallas kernels for 0% -> 0%
where the time goes in v4:
time: 363 us; the launch traced here: 362 us
  waiting for transfers between devices  154 us (42%)
  matrix products  108 us (30%)
  local copies, waits for them, and re-layouts  46.3 us (13%)
  starting transfers between devices  27.7 us (8%)
  between operations  13.9 us (4%)
  other arithmetic  11.7 us (3%)
    all_gather x1, waiting for transfers between devices, on_device(): key_all = lax.all_gather(local_k, 'seq', axis=0, tiled=True)  58.8 us
    reduce_scatter x1, waiting for transfers between devices, on_device(): lax.psum_scatter(key_term.astype(jnp.bfloat16).reshape(seq_total, channel...  57.9 us
    dot_general x1, matrix products, on_device(): jnp.einsum('htu,uhd->thd', dscore, k_heads, preferred_element_type=jnp.fl...  29.1 us
    dot_general x1, matrix products, on_device(): jnp.einsum('htu,thd->uhd', dscore, q_heads, preferred_element_type=jnp.fl...  28.1 us
    ppermute x8, starting transfers between devices, butterfly_sum(): value = value + lax.ppermute(value, axes, pairs)  23.2 us
    sub x1, matrix products, on_device(): raw = jnp.where(visible, jnp.exp(scores - row_top), 0.0)  17.5 us
    ppermute x8, waiting for transfers between devices, butterfly_sum(): value = value + lax.ppermute(value, axes, pairs)  15.1 us
    ppermute x2, waiting for transfers between devices, padded(): after = lax.ppermute(value[:width], 'seq', down)  12.9 us
  transfers between devices with their start and end apart: 16, of which 11 were waited for; matrix products, arithmetic and copies ran while one was open for 46% of the time, Pallas kernels for 0%

profile of v4, /device:TPU:1, one launch (start us, length us, event | category | flops | bytes accessed | tf_op | source)
XLA Modules:
  0.0 362.0 jit_solution(14857884384453621443)
XLA Ops:
  7.2 0.7 all-gather.6.cloned.1.call-update
  7.9 2.0 copy.49
  10.0 58.8 %all-gather.6.cloned.1.call-done = bf16[1,2048,2048]{2,1,0:T(8,128)(2,1)} async-done(((bf16[1,128,2048]{2,1,0:T(8,128)(2,1)}), bf16[1,2048,2048]{2,1,0:T(8,128)(2,1)}) %all-gather.6.cloned.1.call-update) | async-done | bytes 8388624 | tf_op jit(solution)/shard_map/all_gather | solution.py:51
  68.8 1.3 copy.57
  70.1 0.2 slice_bitcast_fusion.1
  70.4 0.3 collective-permute-start.2
  70.7 1.5 collective-permute-start.3
  72.2 0.2 iota_compare_fusion
  72.4 1.2 fusion.68
  73.6 1.3 copy.84
  74.9 9.8 %collective-permute-done.2 = bf16[3,2048]{0,1:T(8,128)(2,1)S(1)} collective-permute-done((bf16[3,2048]{0,1:T(8,128)(2,1)S(1)}, bf16[3,2048]{0,1:T(8,128)(2,1)S(1)}, u32[]{:S(2)}, u32[]{:S(2)}) %collective-permute-start.2) | collective-permute-done | bytes 12320 | tf_op jit(solution)/shard_map/ppermute | solution.py:16
  84.7 3.7 %fusion.44 = bf16[128,2048]{0,1:T(8,128)(2,1)S(1)} fusion(bf16[128,2048]{0,1:T(8,128)(2,1)S(1)} %bitcast.77, bf16[3,2048]{0,1:T(8,128)(2,1)S(1)} %collective-permute-done.3, bf16[3,2048]{0,1:T(8,128)(2,1)S(1)} %collective-permute-done.2, f32[2048]{0:T(1024)S(1)} %bitcast.104, f32[2048]{0:T(1024)S(1)} %bitcast.106, f32[2048]{0:T(1024)S(1)} %bitcast.96, ...), kind=kLoop, calls=%fused_computation.65 | loop fusion | flops 10223616 | bytes 1130496 | tf_op jit(solution)/shard_map/convert_element_type | solution.py:49
  88.4 12.3 %copy.83 = bf16[2048,2048]{0,1:T(8,128)(2,1)} copy(bf16[2048,2048]{1,0:T(8,128)(2,1)} %bitcast.83) | data formatting | bytes 16777216 | tf_op jit(solution)/shard_map/reshape | solution.py:56
  100.8 17.5 %fusion.69 = (f32[16,128]{1,0:T(8,128)S(1)}, f32[16,128,2048]{1,2,0:T(8,128)}) fusion(pred[128,2048]{0,1:T(8,128)(4,1)S(1)} %iota_compare_fusion, bf16[2048,16,128]{0,2,1:T(8,128)(2,1)} %bitcast.81, bf16[128,16,128]{0,2,1:T(8,128)(2,1)S(1)} %bitcast.91), kind=kOutput, calls=%fused_computation.100 | convolution fusion | flops 2172651520 | bytes 25960448 | tf_op jit(solution)/shard_map/sub | solution.py:69
  118.2 11.7 %convolution_convert_fusion = bf16[16,128,2048]{2,1,0:T(8,128)(2,1)} fusion(bf16[128,16,128]{0,2,1:T(8,128)(2,1)S(1)} %bitcast.89, f32[16,128,2048]{1,2,0:T(8,128)} %get-tuple-element.45, f32[16,128]{1,0:T(8,128)S(1)} %get-tuple-element.44), kind=kOutput, calls=%fused_computation.18 | convolution fusion | flops 1086324736 | bytes 25698304 | tf_op jit(solution)/shard_map/htu,thd->uhd/dot_general | solution.py:73
  129.9 12.3 %copy.70 = bf16[2048,2048]{1,0:T(8,128)(2,1)} copy(bf16[2048,2048]{0,1:T(8,128)(2,1)} %bitcast.85) | data formatting | bytes 16777216 | tf_op jit(solution)/shard_map/reshape | solution.py:75
  142.3 0.2 reduce-scatter.3.cloned.1.call-start
  142.5 11.6 %fusion.70 = f32[16,128,2048]{1,2,0:T(8,128)} fusion(bf16[128,16,128]{0,2,1:T(8,128)(2,1)S(1)} %bitcast.90, bf16[2048,16,128]{0,2,1:T(8,128)(2,1)} %bitcast.79), kind=kOutput, calls=%fused_computation.101 | convolution fusion | flops 1073741824 | bytes 25690112 | tf_op jit(solution)/shard_map/thd,uhd->htu/dot_general | solution.py:92
  154.1 28.1 %fusion.18 = bf16[16,2048,128]{1,2,0:T(8,128)(2,1)} fusion(bf16[128,16,128]{0,2,1:T(8,128)(2,1)S(1)} %bitcast.92, f32[16,128,2048]{1,2,0:T(8,128)} %fusion.70, f32[16,128,2048]{1,2,0:T(8,128)} %get-tuple-element.45, f32[16,128]{1,0:T(8,128)S(1)} %get-tuple-element.44), kind=kOutput, calls=%fused_computation.17 | convolution fusion | flops 1107300352 | bytes 42475520 | tf_op jit(solution)/shard_map/htu,thd->uhd/dot_general | solution.py:95
  182.3 12.3 %copy.68 = bf16[2048,2048]{1,0:T(8,128)(2,1)} copy(bf16[2048,2048]{0,1:T(8,128)(2,1)} %bitcast.84) | data formatting | bytes 16777216 | tf_op jit(solution)/shard_map/reshape | solution.py:97
  194.6 0.2 copy.72
  194.8 10.4 %multiply_reduce_fusion.1 = (f32[16,128]{1,0:T(8,128)S(1)}, bf16[128,16,128]{2,0,1:T(8,128)(2,1)S(1)}) fusion(f32[128,16,128]{2,0,1:T(8,128)S(1)} %copy.72, bf16[2048,16,128]{0,2,1:T(8,128)(2,1)} %bitcast.80, f32[16,128,2048]{1,2,0:T(8,128)} %get-tuple-element.45, f32[16,128]{1,0:T(8,128)S(1)} %get-tuple-element.44), kind=kOutput, calls=%fused_computation.72 | convolution fusion | flops 1083176960 | bytes 26755072 | tf_op jit(solution)/shard_map/htu,uhd->thd/dot_general | solution.py:78
  205.3 2.3 collective-permute-start
  207.5 0.3 copy.56
  207.9 0.3 copy.54
  208.2 8.6 %collective-permute-done = bf16[3,2048]{1,0:T(4,128)(2,1)S(1)} collective-permute-done((bf16[3,2048]{1,0:T(4,128)(2,1)S(1)}, bf16[3,2048]{1,0:T(4,128)(2,1)S(1)}, u32[]{:S(2)}, u32[]{:S(2)}) %collective-permute-start) | collective-permute-done | bytes 12320 | tf_op jit(solution)/shard_map/ppermute | solution.py:15
  216.8 0.3 copy.55
  217.1 3.1 collective-permute-done.1
  220.2 3.4 fusion.50
  223.6 0.1 stack.31
  223.8 1.2 collective-permute-done.4
  225.2 4.5 %collective-permute-done.5 = f32[7,2048]{1,0:T(8,128)S(1)} collective-permute-done((f32[7,2048]{1,0:T(8,128)S(1)}, f32[7,2048]{1,0:T(8,128)S(1)}, u32[]{:S(2)}, u32[]{:S(2)}) %collective-permute-start.5) | collective-permute-done | bytes 57376 | tf_op jit(solution)/shard_map/ppermute | solution.py:26
  229.7 3.9 %collective-permute-start.6 = (f32[7,2048]{1,0:T(8,128)S(1)}, f32[7,2048]{1,0:T(8,128)S(1)}, u32[]{:S(2)}, u32[]{:S(2)}) collective-permute-start(f32[7,2048]{1,0:T(8,128)S(1)} %add.89), channel_id=1, source_target_pairs={{0,4},{1,5},{2,6},{3,7},{4,0},{5,1},{6,2},{7,3},{8,12},{9,13},{10,... | collective-permute-start | bytes 172040 | tf_op jit(solution)/shard_map/ppermute | solution.py:26
  233.6 1.9 collective-permute-done.6
  235.5 1.2 collective-permute-start.7
  236.7 3.9 %collective-permute-done.7 = f32[7,2048]{1,0:T(8,128)S(1)} collective-permute-done((f32[7,2048]{1,0:T(8,128)S(1)}, f32[7,2048]{1,0:T(8,128)S(1)}, u32[]{:S(2)}, u32[]{:S(2)}) %collective-permute-start.7) | collective-permute-done | bytes 57376 | tf_op jit(solution)/shard_map/ppermute | solution.py:26
  240.6 4.3 %collective-permute-start.8 = (f32[7,2048]{1,0:T(8,128)S(1)}, f32[7,2048]{1,0:T(8,128)S(1)}, u32[]{:S(2)}, u32[]{:S(2)}) collective-permute-start(f32[7,2048]{1,0:T(8,128)S(1)} %add.91), channel_id=1, source_target_pairs={{0,16},{1,17},{2,18},{3,19},{4,20},{5,21},{6,22},{7,23},{8,24},{9,... | collective-permute-start | bytes 172040 | tf_op jit(solution)/shard_map/ppermute | solution.py:26
  244.9 1.7 collective-permute-done.8
  246.6 2.1 collective-permute-start.9
  248.7 2.0 collective-permute-done.9
  250.7 4.8 %collective-permute-start.10 = (f32[7,2048]{1,0:T(8,128)S(1)}, f32[7,2048]{1,0:T(8,128)S(1)}, u32[]{:S(2)}, u32[]{:S(2)}) collective-permute-start(f32[7,2048]{1,0:T(8,128)S(1)} %add.93), channel_id=1, source_target_pairs={{0,64},{1,65},{2,66},{3,67},{4,68},{5,69},{6,70},{7,71},{8,72},{9,... | collective-permute-start | bytes 172040 | tf_op jit(solution)/shard_map/ppermute | solution.py:26
  255.5 29.1 %fusion.27 = bf16[16,128,128]{2,1,0:T(8,128)(2,1)S(1)} fusion(bf16[2048,16,128]{0,2,1:T(8,128)(2,1)} %bitcast.82, f32[16,128,2048]{1,2,0:T(8,128)} %fusion.70, f32[16,128,2048]{1,2,0:T(8,128)} %get-tuple-element.45, f32[16,128]{1,0:T(8,128)S(1)} %get-tuple-element.44), kind=kOutput, calls=%fused_computation.36 | convolution fusion | flops 1103368192 | bytes 42475520 | tf_op jit(solution)/shard_map/htu,uhd->thd/dot_general | solution.py:100
  284.6 1.0 copy.74
  285.7 6.6 %collective-permute-start.11 = (f32[7,2048]{1,0:T(8,128)S(1)}, f32[7,2048]{1,0:T(8,128)S(1)}, u32[]{:S(2)}, u32[]{:S(2)}) collective-permute-start(f32[7,2048]{1,0:T(8,128)S(1)} %add.94), channel_id=1, source_target_pairs={{0,128},{1,129},{2,130},{3,131},{4,132},{5,133},{6,134},{7,135},{8... | collective-permute-start | bytes 172040 | tf_op jit(solution)/shard_map/ppermute | solution.py:26
  292.2 3.7 %fusion.61 = bf16[1,128,2048]{1,2,0:T(8,128)(2,1)S(1)} fusion(f32[2048]{0:T(1024)S(1)} %bitcast.105, f32[2048]{0:T(1024)S(1)} %bitcast.107, f32[2048]{0:T(1024)S(1)} %bitcast.97, bf16[128,2048]{0,1:T(8,128)(2,1)S(1)} %bitcast.87, f32[2048]{0:T(1024)S(1)} %bitcast.99, f32[2048]{0:T(1024)S(1)} %bitcast.101, f32[2048]{0:T(1024)S(1)} %bitcast.103, ...), kind=kLoop, calls=%fused_computation.89 | loop fusion | flops 10223616 | bytes 1130496 | tf_op jit(solution)/shard_map/broadcast_in_dim | solution.py:103
  296.0 1.0 copy.73
  297.0 0.6 add.95
  297.6 57.9 %reduce-scatter.3.cloned.1.call-done = bf16[128,2048]{1,0:T(8,128)(2,1)} async-done(((bf16[2048,2048]{1,0:T(8,128)(2,1)}), bf16[128,2048]{1,0:T(8,128)(2,1)}) %reduce-scatter.3.cloned.1.call-update) | async-done | bytes 524304 | tf_op jit(solution)/shard_map/reduce_scatter | solution.py:96
  (23 shorter events, 0.5 us)
Async XLA Ops:
  7.2 61.6 %all-gather.6.cloned.1.call-start = ((), (), s32[]{:S(2)}) async-start(), calls=%async_computation.5 | async-start | bytes 8912896 | tf_op jit(solution)/shard_map/all_gather | solution.py:51
  7.9 134.6 %all-gather.4.cloned.1.call-start = ((), (), s32[]{:S(2)}) async-start(), calls=%async_computation.2 | async-start | bytes 8912896 | tf_op jit(solution)/shard_map/all_gather | solution.py:53
  68.8 228.8 %reduce-scatter.5.cloned.1.call-start = ((), (), s32[]{:S(2)}) async-start(), calls=%async_computation.4 | async-start | bytes 8912896 | tf_op jit(solution)/shard_map/reduce_scatter | solution.py:74
  70.4 14.3 %collective-permute-start.2 = (bf16[3,2048]{0,1:T(8,128)(2,1)S(1)}, bf16[3,2048]{0,1:T(8,128)(2,1)S(1)}, u32[]{:S(2)}, u32[]{:S(2)}) collective-permute-start(bf16[3,2048]{0,1:T(8,128)(2,1)S(1)} %get-tuple-element.33), channel_id=1, source_target_pairs={{1,0},{2,1},{3,2},{4,3},{5,4},{6,5},{7,6},{8,7},{9,8},{10,9},{11,1... | collective-permute-start | bytes 36872 | tf_op jit(solution)/shard_map/ppermute | solution.py:16
  70.7 14.0 %collective-permute-start.3 = (bf16[3,2048]{0,1:T(8,128)(2,1)S(1)}, bf16[3,2048]{0,1:T(8,128)(2,1)S(1)}, u32[]{:S(2)}, u32[]{:S(2)}) collective-permute-start(bf16[3,2048]{0,1:T(8,128)(2,1)S(1)} %get-tuple-element.34), channel_id=1, source_target_pairs={{0,1},{1,2},{2,3},{3,4},{4,5},{5,6},{6,7},{7,8},{8,9},{9,10},{10,1... | collective-permute-start | bytes 36872 | tf_op jit(solution)/shard_map/ppermute | solution.py:15
  142.3 213.3 %reduce-scatter.3.cloned.1.call-start = ((), (), s32[]{:S(2)}) async-start(), calls=%async_computation.3 | async-start | bytes 8912896 | tf_op jit(solution)/shard_map/reduce_scatter | solution.py:96
  205.3 11.5 %collective-permute-start = (bf16[3,2048]{1,0:T(4,128)(2,1)S(1)}, bf16[3,2048]{1,0:T(4,128)(2,1)S(1)}, u32[]{:S(2)}, u32[]{:S(2)}) collective-permute-start(bf16[3,2048]{1,0:T(4,128)(2,1)S(1)} %get-tuple-element.36), channel_id=1, source_target_pairs={{0,1},{1,2},{2,3},{3,4},{4,5},{5,6},{6,7},{7,8},{8,9},{9,10},{10,1... | collective-permute-start | bytes 36872 | tf_op jit(solution)/shard_map/ppermute | solution.py:15
  207.8 12.4 %collective-permute-start.1 = (bf16[3,2048]{0,1:T(8,128)(2,1)S(1)}, bf16[3,2048]{0,1:T(8,128)(2,1)S(1)}, u32[]{:S(2)}, u32[]{:S(2)}) collective-permute-start(bf16[3,2048]{0,1:T(8,128)(2,1)S(1)} %copy.56), channel_id=1, source_target_pairs={{1,0},{2,1},{3,2},{4,3},{5,4},{6,5},{7,6},{8,7},{9,8},{10,9},{11,1... | collective-permute-start | bytes 36872 | tf_op jit(solution)/shard_map/ppermute | solution.py:16
  223.7 1.3 collective-permute-start.4
  225.1 4.6 %collective-permute-start.5 = (f32[7,2048]{1,0:T(8,128)S(1)}, f32[7,2048]{1,0:T(8,128)S(1)}, u32[]{:S(2)}, u32[]{:S(2)}) collective-permute-start(f32[7,2048]{1,0:T(8,128)S(1)} %add.88), channel_id=1, source_target_pairs={{0,2},{1,3},{2,0},{3,1},{4,6},{5,7},{6,4},{7,5},{8,10},{9,11},{10,... | collective-permute-start | bytes 172040 | tf_op jit(solution)/shard_map/ppermute | solution.py:26
  229.7 5.8 %collective-permute-start.6 = (f32[7,2048]{1,0:T(8,128)S(1)}, f32[7,2048]{1,0:T(8,128)S(1)}, u32[]{:S(2)}, u32[]{:S(2)}) collective-permute-start(f32[7,2048]{1,0:T(8,128)S(1)} %add.89), channel_id=1, source_target_pairs={{0,4},{1,5},{2,6},{3,7},{4,0},{5,1},{6,2},{7,3},{8,12},{9,13},{10,... | collective-permute-start | bytes 172040 | tf_op jit(solution)/shard_map/ppermute | solution.py:26
  235.5 5.1 %collective-permute-start.7 = (f32[7,2048]{1,0:T(8,128)S(1)}, f32[7,2048]{1,0:T(8,128)S(1)}, u32[]{:S(2)}, u32[]{:S(2)}) collective-permute-start(f32[7,2048]{1,0:T(8,128)S(1)} %add.90), channel_id=1, source_target_pairs={{0,8},{1,9},{2,10},{3,11},{4,12},{5,13},{6,14},{7,15},{8,0},{9,1},... | collective-permute-start | bytes 172040 | tf_op jit(solution)/shard_map/ppermute | solution.py:26
  240.6 6.0 %collective-permute-start.8 = (f32[7,2048]{1,0:T(8,128)S(1)}, f32[7,2048]{1,0:T(8,128)S(1)}, u32[]{:S(2)}, u32[]{:S(2)}) collective-permute-start(f32[7,2048]{1,0:T(8,128)S(1)} %add.91), channel_id=1, source_target_pairs={{0,16},{1,17},{2,18},{3,19},{4,20},{5,21},{6,22},{7,23},{8,24},{9,... | collective-permute-start | bytes 172040 | tf_op jit(solution)/shard_map/ppermute | solution.py:26
  246.6 4.1 %collective-permute-start.9 = (f32[7,2048]{1,0:T(8,128)S(1)}, f32[7,2048]{1,0:T(8,128)S(1)}, u32[]{:S(2)}, u32[]{:S(2)}) collective-permute-start(f32[7,2048]{1,0:T(8,128)S(1)} %add.92), channel_id=1, source_target_pairs={{0,32},{1,33},{2,34},{3,35},{4,36},{5,37},{6,38},{7,39},{8,40},{9,... | collective-permute-start | bytes 172040 | tf_op jit(solution)/shard_map/ppermute | solution.py:26
  250.7 34.9 %collective-permute-start.10 = (f32[7,2048]{1,0:T(8,128)S(1)}, f32[7,2048]{1,0:T(8,128)S(1)}, u32[]{:S(2)}, u32[]{:S(2)}) collective-permute-start(f32[7,2048]{1,0:T(8,128)S(1)} %add.93), channel_id=1, source_target_pairs={{0,64},{1,65},{2,66},{3,67},{4,68},{5,69},{6,70},{7,71},{8,72},{9,... | collective-permute-start | bytes 172040 | tf_op jit(solution)/shard_map/ppermute | solution.py:26
  285.7 11.3 %collective-permute-start.11 = (f32[7,2048]{1,0:T(8,128)S(1)}, f32[7,2048]{1,0:T(8,128)S(1)}, u32[]{:S(2)}, u32[]{:S(2)}) collective-permute-start(f32[7,2048]{1,0:T(8,128)S(1)} %add.94), channel_id=1, source_target_pairs={{0,128},{1,129},{2,130},{3,131},{4,132},{5,133},{6,134},{7,135},{8... | collective-permute-start | bytes 172040 | tf_op jit(solution)/shard_map/ppermute | solution.py:26
Sparse Core Ops, SparseCore 0:
  9.9 58.8 all-gather.5
  71.1 67.2 all-gather.3
  142.4 108.4 reduce-scatter.4
  253.9 101.5 reduce-scatter.2
